TPU v7x, 128 devices: a whole 4x4x4 slice. The times are simulated.
128 devices in a mesh: gx: 4 (over z), gy: 16 (over x, y_lo, core), gz: 2 (over y_hi).
Axes of the slice: x: 4, y: 4 (y_hi: 2, y_lo: 2; y = y_hi * 2 + y_lo), z: 4, core: 2. Of those that a mesh axis runs over, the one named last changes fastest.
Arguments:
- right_side: float32 [64, 1024, 512], P('gx', 'gy', 'gz'), may hold values from -4 to 4
- initial_guess: float32 [64, 1024, 512], P('gx', 'gy', 'gz'), may hold values from -3 to 3
- damping: float32 [64, 1024, 512], P('gx', 'gy', 'gz'), may hold values from 0.1 to 4
- group_map: int32 [16, 256, 128], P('gx', 'gy', 'gz'), may hold values from 0 to 1023
- block_inverse: float32 [1024, 1024], P('gy'), may hold values from -0.1875 to 0.1875
Outputs:
- fine_iterate: float32 [64, 1024, 512], P('gx', 'gy', 'gz')
- middle_correction: float32 [32, 512, 256], P('gx', 'gy', 'gz')
- coarse_correction: float32 [16, 256, 128], P('gx', 'gy', 'gz')
- aggregate_solution: float32 [1024], P('gy')
All inputs are finite; a program needn't handle non-finite values.
Results may differ from a plain program's by a relative error of at most 0.0003.
Values sent between devices are 32-bit elements; how exact they have to be, the bound alone decides.
No kernel may reach another device: no remote copies, remote signals or barrier semaphores. Data moves between devices by JAX's collectives and lax.ppermute only.
A program may use at most 192 MiB of HBM per device.

v0:
```python
import math

import jax
import jax.numpy as jnp
from jax import lax
from jax.sharding import PartitionSpec as P

SWEEPS = 4
NAGG = 1024


OMEGA = 0.8


def with_halo(cells, sides, width):
    for axis, dim in sides:
        count = lax.axis_size(axis)
        ends = count - 1
        head = lax.slice_in_dim(cells, 0, width, axis=dim)
        tail = lax.slice_in_dim(cells, cells.shape[dim] - width, cells.shape[dim], axis=dim)
        cells = jnp.concatenate(
            [
                lax.ppermute(tail, axis, [(i, (i + 1) % count) for i in range(ends)]),
                cells,
                lax.ppermute(head, axis, [((i + 1) % count, i) for i in range(ends)]),
            ],
            axis=dim,
        )
    return cells


def neighbours(padded):
    total = padded[2:, 1:-1, 1:-1] + padded[:-2, 1:-1, 1:-1]
    total = total + padded[1:-1, 2:, 1:-1] + padded[1:-1, :-2, 1:-1]
    return total + padded[1:-1, 1:-1, 2:] + padded[1:-1, 1:-1, :-2]


def relax(padded, source, diagonal):
    centre = padded[1:-1, 1:-1, 1:-1]
    return centre + OMEGA * (source - (diagonal * centre - neighbours(padded))) / diagonal


def defect(padded, source, diagonal):
    centre = padded[1:-1, 1:-1, 1:-1]
    return source - (diagonal * centre - neighbours(padded))


def shrink(field):
    extent_a, extent_b, extent_c = field.shape
    blocks = field.reshape(extent_a // 2, 2, extent_b // 2, 2, extent_c // 2, 2)
    return blocks.sum(axis=(1, 3, 5)) * 0.125


def fine_rim(field):
    return with_halo(field, (("gx", 0), ("gy", 1), ("gz", 2)), 1)


def middle_rim(field):
    return with_halo(field, (("gx", 0), ("gy", 1), ("gz", 2)), 1)


def coarse_rim(field):
    return with_halo(field, (("gx", 0), ("gy", 1), ("gz", 2)), 1)


def shards(right_side, initial_guess, damping, group_map, block_inverse):
    fine_diag = 6.0 + damping
    iterate = initial_guess
    for sweep_count in range(SWEEPS):
        iterate = relax(fine_rim(iterate), right_side, fine_diag)
    fine_defect = defect(fine_rim(iterate), right_side, fine_diag)
    middle_damp = 4.0 * shrink(damping)
    middle_source = 4.0 * shrink(fine_defect)
    middle_diag = 6.0 + middle_damp
    middle = OMEGA * middle_source / middle_diag
    for sweep_count in range(SWEEPS - 1):
        middle = relax(middle_rim(middle), middle_source, middle_diag)
    middle_defect = defect(middle_rim(middle), middle_source, middle_diag)
    coarse_damp = 4.0 * shrink(middle_damp)
    coarse_source = 4.0 * shrink(middle_defect)
    coarse_diag = 6.0 + coarse_damp
    coarse = OMEGA * coarse_source / coarse_diag
    for sweep_count in range(SWEEPS - 1):
        coarse = relax(coarse_rim(coarse), coarse_source, coarse_diag)
    coarse_defect = defect(coarse_rim(coarse), coarse_source, coarse_diag)
    partial_sums = jax.ops.segment_sum(
        coarse_defect.reshape(-1), group_map.reshape(-1), num_segments=NAGG
    )
    summed = lax.psum(partial_sums, ("gx", "gy", "gz"))
    group_cells = (
        coarse_source.size * lax.axis_size("gx") * lax.axis_size("gy") * lax.axis_size("gz") // NAGG
    )
    aggregate_source = summed / math.sqrt(group_cells)
    solution = jnp.dot(block_inverse, aggregate_source, precision=lax.Precision.HIGHEST)
    return (iterate, middle, coarse, solution)


def solution(mesh):
    return jax.shard_map(
        shards,
        mesh=mesh,
        in_specs=(
            P("gx", "gy", "gz"),
            P("gx", "gy", "gz"),
            P("gx", "gy", "gz"),
            P("gx", "gy", "gz"),
            P("gy", None),
        ),
        out_specs=(P("gx", "gy", "gz"), P("gx", "gy", "gz"), P("gx", "gy", "gz"), P("gy")),
        check_vma=False,
    )
```

profile of v0, /device:TPU:1, one launch (start us, length us, event | category | flops | bytes accessed | tf_op | source)
XLA Modules:
  0.0 835.7 jit_solution(205447732335206814)
XLA Ops:
  51.7 20.5 %fusion.42 = f32[16,64,256]{1,0,2:T(8,128)S(1)} fusion(f32[16,64,256]{1,0,2:T(8,128)} %copy.173, f32[16,64,256]{1,0,2:T(8,128)} %copy.172, f32[18,66,1]{1,0,2:T(8,128)S(1)} %collective-permute-done.5, f32[18,1,256]{1,0,2:T(8,128)} %copy.165, f32[18,64,256]{1,0,2:T(8,128)} %copy-done.15, f32[18,1,256]{1,0,2:T(8,128)} %copy.167, ...), kind=kLoop, calls=%fused_computation.120 | loop fusion | flops 5242880 | bytes 7517472 | tf_op jit(solution)/shard_map/add | solution.py:40
  119.8 10.3 %fusion.32 = f32[16,64,256]{1,0,2:T(8,128)S(1)} fusion(f32[16,64,256]{1,0,2:T(8,128)S(1)} %copy-done.7, f32[16,64,256]{1,0,2:T(8,128)S(1)} %copy-done.1, f32[18,66,1]{1,0,2:T(8,128)S(1)} %collective-permute-done.11, f32[18,1,256]{1,0,2:T(8,128)} %copy.181, f32[18,1,256]{1,0,2:T(8,128)S(1)} %copy-done.12, f32[1,64,256]{1,0,2:T(1,128)S(1)} %copy.175, ...), kind=kLoop, calls=%fused_computation.92 | loop fusion | flops 7864320 | bytes 4371744 | tf_op jit(solution)/shard_map/add | solution.py:40
  172.0 5.8 collective-permute-start.17
  178.7 10.3 %fusion.22 = f32[16,64,256]{1,0,2:T(8,128)S(1)} fusion(f32[16,64,256]{1,0,2:T(8,128)S(1)} %copy-done.9, f32[16,64,256]{1,0,2:T(8,128)S(1)} %copy-done.2, f32[18,66,1]{1,0,2:T(8,128)S(1)} %collective-permute-done.17, f32[18,1,256]{1,0,2:T(8,128)} %copy.194, f32[18,1,256]{1,0,2:T(8,128)S(1)} %copy-done.13, f32[1,64,256]{1,0,2:T(1,128)S(1)} %copy.188, ...), kind=kLoop, calls=%fused_computation.64 | loop fusion | flops 7864320 | bytes 4371744 | tf_op jit(solution)/shard_map/add | solution.py:40
  194.8 5.5 collective-permute-start.19
  230.4 6.3 collective-permute-start.23
  237.6 10.3 %fusion.12 = f32[16,64,256]{1,0,2:T(8,128)S(1)} fusion(f32[16,64,256]{1,0,2:T(8,128)S(1)} %copy-done.11, f32[16,64,256]{1,0,2:T(8,128)S(1)} %copy-done.3, f32[18,66,1]{1,0,2:T(8,128)S(1)} %collective-permute-done.23, f32[18,1,256]{1,0,2:T(8,128)} %copy.207, f32[18,1,256]{1,0,2:T(8,128)S(1)} %copy-done.14, f32[1,64,256]{1,0,2:T(1,128)S(1)} %copy.201, ...), kind=kLoop, calls=%fused_computation.36 | loop fusion | flops 7864320 | bytes 4371744 | tf_op jit(solution)/shard_map/add | solution.py:40
  288.8 7.2 collective-permute-start.29
  296.0 68.4 %reshape.25 = f32[8,2,32,2,128,2]{5,4,3,2,1,0:T(8,128)} reshape(f32[16,64,256]{2,1,0:T(8,128)S(1)} %copy-done.16) | data formatting | bytes 2097152 | tf_op jit(solution)/shard_map/reshape | solution.py:50
  364.4 20.8 %reduce_sum.37 = f32[8,32,128]{2,1,0:T(8,128)S(1)} reduce(f32[8,2,32,2,128,2]{5,4,3,2,1,0:T(8,128)} %reshape.25, f32[]{:T(128)} %constant.9.clone.1), dimensions={1,3,5}, to_apply=%region_1.0 | reduce | flops 229376 | bytes 1179652 | tf_op jit(solution)/shard_map/reduce_sum | solution.py:51
  385.3 22.7 %fusion.2 = f32[16,64,256]{1,0,2:T(8,128)} fusion(f32[16,64,256]{1,0,2:T(8,128)} %copy.172, f32[18,66,1]{1,0,2:T(8,128)} %collective-permute-done.29, f32[18,1,256]{1,0,2:T(8,128)} %copy.220, f32[18,1,256]{1,0,2:T(8,128)} %copy.222, f32[1,64,256]{1,0,2:T(1,128)S(1)} %copy.214, f32[16,64,256]{1,0,2:T(8,128)} %copy-done.4, f32[1,64,256]{1,0,2:T(1,128)S(1)} %copy-done.18, ...), kind=kLoop, calls=%fused_computation.8 | loop fusion | flops 7077888 | bytes 4371744 | tf_op jit(solution)/shard_map/sub | solution.py:45
  410.5 68.4 %reshape.24 = f32[8,2,32,2,128,2]{5,4,3,2,1,0:T(8,128)} reshape(f32[16,64,256]{2,1,0:T(8,128)S(1)} %copy.226) | data formatting | bytes 2097152 | tf_op jit(solution)/shard_map/reshape | solution.py:50
  478.9 20.8 %reduce_sum.36 = f32[8,32,128]{2,1,0:T(8,128)S(1)} reduce(f32[8,2,32,2,128,2]{5,4,3,2,1,0:T(8,128)} %reshape.24, f32[]{:T(128)} %constant.9.clone.1), dimensions={1,3,5}, to_apply=%region_0.0 | reduce | flops 229376 | bytes 1179652 | tf_op jit(solution)/shard_map/reduce_sum | solution.py:51
  519.8 5.5 collective-permute-start.35
  550.0 6.2 collective-permute-start.41
  578.3 6.2 collective-permute-start.47
  605.5 6.4 collective-permute-start.53
  611.9 9.8 %mul.126 = f32[4,2,16,2,64,2]{5,4,3,2,1,0:T(8,128)} reshape(f32[8,32,128]{2,1,0:T(8,128)S(1)} %get-tuple-element.65) | data formatting | bytes 262144 | tf_op jit(solution)/shard_map/mul | solution.py:72
  625.9 9.8 %reshape.26 = f32[4,2,16,2,64,2]{5,4,3,2,1,0:T(8,128)} reshape(f32[8,32,128]{2,1,0:T(8,128)S(1)} %fusion.48) | data formatting | bytes 262144 | tf_op jit(solution)/shard_map/reshape | solution.py:50
  681.1 6.1 collective-permute-start.65
  705.9 6.1 collective-permute-start.71
  730.7 6.1 collective-permute-start.77
  739.1 28.8 %scatter_custom_fusion = f32[1024]{0:T(1024)S(1)} fusion(s32[4096]{0:T(1024)S(1)} %reshape.30, f32[4096]{0:T(1024)S(1)} %reshape.32, f32[]{:T(128)} %constant.9.clone.1), kind=kCustom, calls=%fused_computation.415 | custom fusion | flops 4096 | bytes 4100 | tf_op jit(solution)/shard_map/scatter-add | solution.py:86
  767.9 66.8 %psum.7 = f32[1024]{0:T(1024)S(1)} all-reduce(f32[1024]{0:T(1024)S(1)} %scatter_custom_fusion), channel_id=1, replica_groups=mesh['gx'=4,'gy'=16,'gz'=2] {'gx','gy','gz'}, use_global_device_ids=true, to_apply=%region_5.0 | all-reduce | flops 1024 | bytes 8192 | tf_op jit(solution)/shard_map/psum | solution.py:89
  (311 shorter events, 398.2 us)
Async XLA Ops:
  14.9 9.2 %collective-permute-start.3 = (f32[18,1,256]{2,0,1:T(8,128)S(1)}, f32[18,1,256]{2,0,1:T(8,128)S(1)}, u32[]{:S(2)}, u32[]{:S(2)}) collective-permute-start(f32[18,1,256]{2,0,1:T(8,128)S(1)} %copy.231), channel_id=1, source_target_pairs={{0,2},{2,4},{4,6},{6,8},{8,10},{10,12},{12,14},{14,16},{16,18},{18... | collective-permute-start | bytes 55304 | tf_op jit(solution)/shard_map/ppermute | solution.py:23
  29.8 21.9 %collective-permute-start.4 = (f32[18,66,1]{1,0,2:T(8,128)S(1)}, f32[18,66,1]{1,0,2:T(8,128)S(1)}, u32[]{:S(2)}, u32[]{:S(2)}) collective-permute-start(f32[18,66,1]{1,0,2:T(8,128)S(1)} %get-tuple-element.16), channel_id=1, source_target_pairs={{1,0},{3,2},{5,4},{7,6},{9,8},{11,10},{13,12},{15,14},{17,16},{19,... | collective-permute-start | bytes 14264 | tf_op jit(solution)/shard_map/ppermute | solution.py:25
  31.2 20.5 %collective-permute-start.5 = (f32[18,66,1]{1,0,2:T(8,128)S(1)}, f32[18,66,1]{1,0,2:T(8,128)S(1)}, u32[]{:S(2)}, u32[]{:S(2)}) collective-permute-start(f32[18,66,1]{1,0,2:T(8,128)S(1)} %get-tuple-element.17), channel_id=1, source_target_pairs={{0,1},{2,3},{4,5},{6,7},{8,9},{10,11},{12,13},{14,15},{16,17},{18,... | collective-permute-start | bytes 14264 | tf_op jit(solution)/shard_map/ppermute | solution.py:23
  94.3 10.2 %collective-permute-start.9 = (f32[18,1,256]{2,0,1:T(8,128)}, f32[18,1,256]{2,0,1:T(8,128)}, u32[]{:S(2)}, u32[]{:S(2)}) collective-permute-start(f32[18,1,256]{2,0,1:T(8,128)} %copy.182), channel_id=1, source_target_pairs={{0,2},{2,4},{4,6},{6,8},{8,10},{10,12},{12,14},{14,16},{16,18},{18... | collective-permute-start | bytes 55304 | tf_op jit(solution)/shard_map/ppermute | solution.py:23
  152.7 10.3 %collective-permute-start.15 = (f32[18,1,256]{2,0,1:T(8,128)}, f32[18,1,256]{2,0,1:T(8,128)}, u32[]{:S(2)}, u32[]{:S(2)}) collective-permute-start(f32[18,1,256]{2,0,1:T(8,128)} %copy.195), channel_id=1, source_target_pairs={{0,2},{2,4},{4,6},{6,8},{8,10},{10,12},{12,14},{14,16},{16,18},{18... | collective-permute-start | bytes 55304 | tf_op jit(solution)/shard_map/ppermute | solution.py:23
  192.8 7.5 collective-permute-start.18
  211.7 9.7 %collective-permute-start.21 = (f32[18,1,256]{2,0,1:T(8,128)}, f32[18,1,256]{2,0,1:T(8,128)}, u32[]{:S(2)}, u32[]{:S(2)}) collective-permute-start(f32[18,1,256]{2,0,1:T(8,128)} %copy.208), channel_id=1, source_target_pairs={{0,2},{2,4},{4,6},{6,8},{8,10},{10,12},{12,14},{14,16},{16,18},{18... | collective-permute-start | bytes 55304 | tf_op jit(solution)/shard_map/ppermute | solution.py:23
  228.9 7.9 collective-permute-start.22
  270.4 9.2 %collective-permute-start.27 = (f32[18,1,256]{2,0,1:T(8,128)}, f32[18,1,256]{2,0,1:T(8,128)}, u32[]{:S(2)}, u32[]{:S(2)}) collective-permute-start(f32[18,1,256]{2,0,1:T(8,128)} %copy.221), channel_id=1, source_target_pairs={{0,2},{2,4},{4,6},{6,8},{8,10},{10,12},{12,14},{14,16},{16,18},{18... | collective-permute-start | bytes 55304 | tf_op jit(solution)/shard_map/ppermute | solution.py:23
  287.5 97.7 %collective-permute-start.28 = (f32[18,66,1]{1,0,2:T(8,128)}, f32[18,66,1]{1,0,2:T(8,128)S(1)}, u32[]{:S(2)}, u32[]{:S(2)}) collective-permute-start(f32[18,66,1]{1,0,2:T(8,128)} %get-tuple-element.18), channel_id=1, source_target_pairs={{1,0},{3,2},{5,4},{7,6},{9,8},{11,10},{13,12},{15,14},{17,16},{19,... | collective-permute-start | bytes 14264 | tf_op jit(solution)/shard_map/ppermute | solution.py:25
  288.8 96.5 %collective-permute-start.29 = (f32[18,66,1]{1,0,2:T(8,128)}, f32[18,66,1]{1,0,2:T(8,128)}, u32[]{:S(2)}, u32[]{:S(2)}) collective-permute-start(f32[18,66,1]{1,0,2:T(8,128)} %get-tuple-element.19), channel_id=1, source_target_pairs={{0,1},{2,3},{4,5},{6,7},{8,9},{10,11},{12,13},{14,15},{16,17},{18,... | collective-permute-start | bytes 14264 | tf_op jit(solution)/shard_map/ppermute | solution.py:23
  518.5 8.8 %collective-permute-start.34 = (f32[10,34,1]{2,1,0:T(8,128)S(1)}, f32[10,34,1]{2,1,0:T(8,128)S(1)}, u32[]{:S(2)}, u32[]{:S(2)}) collective-permute-start(f32[10,34,1]{2,1,0:T(8,128)S(1)} %get-tuple-element.55), channel_id=1, source_target_pairs={{1,0},{3,2},{5,4},{7,6},{9,8},{11,10},{13,12},{15,14},{17,16},{19,... | collective-permute-start | bytes 4088 | tf_op jit(solution)/shard_map/ppermute | solution.py:25
  519.8 9.3 %collective-permute-start.35 = (f32[10,34,1]{2,1,0:T(8,128)S(1)}, f32[10,34,1]{2,1,0:T(8,128)S(1)}, u32[]{:S(2)}, u32[]{:S(2)}) collective-permute-start(f32[10,34,1]{2,1,0:T(8,128)S(1)} %get-tuple-element.56), channel_id=1, source_target_pairs={{0,1},{2,3},{4,5},{6,7},{8,9},{10,11},{12,13},{14,15},{16,17},{18,... | collective-permute-start | bytes 4088 | tf_op jit(solution)/shard_map/ppermute | solution.py:23
  538.1 7.4 collective-permute-start.39
  548.7 9.3 %collective-permute-start.40 = (f32[10,34,1]{2,1,0:T(8,128)S(1)}, f32[10,34,1]{2,1,0:T(8,128)S(1)}, u32[]{:S(2)}, u32[]{:S(2)}) collective-permute-start(f32[10,34,1]{2,1,0:T(8,128)S(1)} %get-tuple-element.53), channel_id=1, source_target_pairs={{1,0},{3,2},{5,4},{7,6},{9,8},{11,10},{13,12},{15,14},{17,16},{19,... | collective-permute-start | bytes 4088 | tf_op jit(solution)/shard_map/ppermute | solution.py:25
  550.0 9.7 %collective-permute-start.41 = (f32[10,34,1]{2,1,0:T(8,128)S(1)}, f32[10,34,1]{2,1,0:T(8,128)S(1)}, u32[]{:S(2)}, u32[]{:S(2)}) collective-permute-start(f32[10,34,1]{2,1,0:T(8,128)S(1)} %get-tuple-element.54), channel_id=1, source_target_pairs={{0,1},{2,3},{4,5},{6,7},{8,9},{10,11},{12,13},{14,15},{16,17},{18,... | collective-permute-start | bytes 4088 | tf_op jit(solution)/shard_map/ppermute | solution.py:23
  577.0 9.3 %collective-permute-start.46 = (f32[10,34,1]{2,1,0:T(8,128)S(1)}, f32[10,34,1]{2,1,0:T(8,128)S(1)}, u32[]{:S(2)}, u32[]{:S(2)}) collective-permute-start(f32[10,34,1]{2,1,0:T(8,128)S(1)} %get-tuple-element.51), channel_id=1, source_target_pairs={{1,0},{3,2},{5,4},{7,6},{9,8},{11,10},{13,12},{15,14},{17,16},{19,... | collective-permute-start | bytes 4088 | tf_op jit(solution)/shard_map/ppermute | solution.py:25
  578.3 9.7 %collective-permute-start.47 = (f32[10,34,1]{2,1,0:T(8,128)S(1)}, f32[10,34,1]{2,1,0:T(8,128)S(1)}, u32[]{:S(2)}, u32[]{:S(2)}) collective-permute-start(f32[10,34,1]{2,1,0:T(8,128)S(1)} %get-tuple-element.52), channel_id=1, source_target_pairs={{0,1},{2,3},{4,5},{6,7},{8,9},{10,11},{12,13},{14,15},{16,17},{18,... | collective-permute-start | bytes 4088 | tf_op jit(solution)/shard_map/ppermute | solution.py:23
  604.2 21.5 %collective-permute-start.52 = (f32[10,34,1]{2,1,0:T(8,128)S(1)}, f32[10,34,1]{2,1,0:T(8,128)S(1)}, u32[]{:S(2)}, u32[]{:S(2)}) collective-permute-start(f32[10,34,1]{2,1,0:T(8,128)S(1)} %get-tuple-element.49), channel_id=1, source_target_pairs={{1,0},{3,2},{5,4},{7,6},{9,8},{11,10},{13,12},{15,14},{17,16},{19,... | collective-permute-start | bytes 4088 | tf_op jit(solution)/shard_map/ppermute | solution.py:25
  605.5 20.2 %collective-permute-start.53 = (f32[10,34,1]{2,1,0:T(8,128)S(1)}, f32[10,34,1]{2,1,0:T(8,128)S(1)}, u32[]{:S(2)}, u32[]{:S(2)}) collective-permute-start(f32[10,34,1]{2,1,0:T(8,128)S(1)} %get-tuple-element.50), channel_id=1, source_target_pairs={{0,1},{2,3},{4,5},{6,7},{8,9},{10,11},{12,13},{14,15},{16,17},{18,... | collective-permute-start | bytes 4088 | tf_op jit(solution)/shard_map/ppermute | solution.py:23
  681.1 7.5 collective-permute-start.65
  705.9 7.5 collective-permute-start.71
  729.4 9.5 %collective-permute-start.76 = (f32[6,18,1]{2,1,0:T(8,128)S(1)}, f32[6,18,1]{2,1,0:T(8,128)S(1)}, u32[]{:S(2)}, u32[]{:S(2)}) collective-permute-start(f32[6,18,1]{2,1,0:T(8,128)S(1)} %get-tuple-element.75), channel_id=1, source_target_pairs={{1,0},{3,2},{5,4},{7,6},{9,8},{11,10},{13,12},{15,14},{17,16},{19,... | collective-permute-start | bytes 1304 | tf_op jit(solution)/shard_map/ppermute | solution.py:25
  730.7 8.2 collective-permute-start.77
  (80 other events, 1649.7 us)
where the time goes:
time: 847 us; the launch traced here: 836 us
  local copies, waits for them, and re-layouts  275 us (32%)
  starting transfers between devices  245 us (29%)
  other arithmetic  172 us (20%)
  waiting for transfers between devices  74.5 us (9%)
  blocking collectives  66.8 us (8%)
    ppermute x39, starting transfers between devices, with_halo(): lax.ppermute(tail, axis, [(i, (i + 1) % count) for i in range(ends)])  186 us
    reshape x3, local copies, waits for them, and re-layouts, shrink(): blocks = field.reshape(extent_a // 2, 2, extent_b // 2, 2, extent_c // 2, 2)  147 us
    psum x1, blocking collectives, shards(): summed = lax.psum(partial_sums, ('gx', 'gy', 'gz'))  66.8 us
    ppermute x39, waiting for transfers between devices, with_halo(): lax.ppermute(head, axis, [((i + 1) % count, i) for i in range(ends)])  62.3 us
    ppermute x39, starting transfers between devices, with_halo(): lax.ppermute(head, axis, [((i + 1) % count, i) for i in range(ends)])  59.4 us
    add x10, other arithmetic, relax(): centre + OMEGA * (source - (diagonal * centre - neighbours(padded))) / di...  52.3 us
    reduce_sum x4, other arithmetic, shrink(): return blocks.sum(axis=(1, 3, 5)) * 0.125  49.6 us
    slice x25, local copies, waits for them, and re-layouts, with_halo(): lax.slice_in_dim(cells, cells.shape[dim] - width, cells.shape[dim], axis=...  32.6 us
  transfers between devices with their start and end apart: 78, of which 36 were waited for; matrix products, arithmetic and copies ran while one was open for 19% of the time, Pallas kernels for 0%

commit v1 on v0

--- a/solution.py
+++ b/solution.py
@@ -45,10 +45,22 @@
     return source - (diagonal * centre - neighbours(padded))
 
 
+def pair_matrix(rows, cols, along):
+    row = lax.broadcasted_iota(jnp.int32, (rows, cols), 0)
+    col = lax.broadcasted_iota(jnp.int32, (rows, cols), 1)
+    if along == 0:
+        return (col // 2 == row).astype(jnp.float32)
+    return (row // 2 == col).astype(jnp.float32)
+
+
 def shrink(field):
     extent_a, extent_b, extent_c = field.shape
-    blocks = field.reshape(extent_a // 2, 2, extent_b // 2, 2, extent_c // 2, 2)
-    return blocks.sum(axis=(1, 3, 5)) * 0.125
+    halves = field.reshape(extent_a // 2, 2, extent_b, extent_c)
+    flat = (halves[:, 0] + halves[:, 1]).reshape(extent_a // 2 * extent_b, extent_c)
+    rows = extent_a // 2 * extent_b
+    flat = jnp.dot(pair_matrix(rows // 2, rows, 0), flat, precision=lax.Precision.HIGHEST)
+    flat = jnp.dot(flat, pair_matrix(extent_c, extent_c // 2, 1), precision=lax.Precision.HIGHEST)
+    return flat.reshape(extent_a // 2, extent_b // 2, extent_c // 2) * 0.125
 
 
 def fine_rim(field):
@@ -83,9 +95,13 @@
     for sweep_count in range(SWEEPS - 1):
         coarse = relax(coarse_rim(coarse), coarse_source, coarse_diag)
     coarse_defect = defect(coarse_rim(coarse), coarse_source, coarse_diag)
-    partial_sums = jax.ops.segment_sum(
-        coarse_defect.reshape(-1), group_map.reshape(-1), num_segments=NAGG
-    )
+    cells = coarse_defect.size
+    one_hot = (
+        group_map.reshape(cells, 1) == lax.broadcasted_iota(jnp.int32, (cells, NAGG), 1)
+    ).astype(jnp.float32)
+    partial_sums = jnp.dot(
+        coarse_defect.reshape(1, cells), one_hot, precision=lax.Precision.HIGHEST
+    ).reshape(NAGG)
     summed = lax.psum(partial_sums, ("gx", "gy", "gz"))
     group_cells = (
         coarse_source.size * lax.axis_size("gx") * lax.axis_size("gy") * lax.axis_size("gz") // NAGG

time: 847 us -> 479 us (0.57)
  local copies, waits for them, and re-layouts: 275 us -> 43.5 us
  other arithmetic: 172 us -> 29.4 us
  waiting for transfers between devices: 74.5 us -> 38.2 us
  starting transfers between devices: 245 us -> 274 us
  matrix products: 0.84 us -> 11.7 us
  blocking collectives: 66.8 us -> 76.4 us
    reshape x4 -> x1, local copies, waits for them, and re-layouts: 147 us -> 0.09 us  [the longest x3 147 us: shrink(): blocks = field.reshape(extent_a // 2, 2, extent_b // 2, 2, extent_c // 2, 2)]
    ppermute x39, waiting for transfers between devices: 62.3 us -> 7.18 us  [with_halo(): lax.ppermute(head, axis, [((i + 1) % count, i) for i in range(ends)])]
    reduce_sum x4 -> x0, other arithmetic: 49.6 us -> none  [shrink(): return blocks.sum(axis=(1, 3, 5)) * 0.125]
    add x10, other arithmetic: 52.3 us -> 22.4 us  [relax(): centre + OMEGA * (source - (diagonal * centre - neighbours(padded))) / di...]
    scatter-add x1 -> x0, other arithmetic: 28.8 us -> none  [shards(): jax.ops.segment_sum(coarse_defect.reshape(-1), group_map.reshape(-1), num...]
    ppermute x39, starting transfers between devices: 186 us -> 213 us  [with_halo(): lax.ppermute(tail, axis, [(i, (i + 1) % count) for i in range(ends)])]
    slice x25 -> x18, local copies, waits for them, and re-layouts: 32.6 us -> 7.46 us  [with_halo(): lax.slice_in_dim(cells, cells.shape[dim] - width, cells.shape[dim], axis=...]
    unnamed x61 -> x64, local copies, waits for them, and re-layouts: 22.5 us -> 3.25 us
  transfers between devices with their start and end apart: 78 -> 78, of which waited for: 36 -> 39; matrix products, arithmetic and copies ran while one was open for 19% -> 5% of each run, Pallas kernels for 0% -> 0%
where the time goes in v1:
time: 479 us; the launch traced here: 476 us
  starting transfers between devices  274 us (57%)
  blocking collectives  76.4 us (16%)
  local copies, waits for them, and re-layouts  43.5 us (9%)
  waiting for transfers between devices  38.2 us (8%)
  other arithmetic  29.4 us (6%)
  matrix products  11.7 us (2%)
    ppermute x39, starting transfers between devices, with_halo(): lax.ppermute(tail, axis, [(i, (i + 1) % count) for i in range(ends)])  213 us
    psum x1, blocking collectives, shards(): summed = lax.psum(partial_sums, ('gx', 'gy', 'gz'))  76.4 us
    ppermute x39, starting transfers between devices, with_halo(): lax.ppermute(head, axis, [((i + 1) % count, i) for i in range(ends)])  61.4 us
    ppermute x39, waiting for transfers between devices, with_halo(): lax.ppermute(tail, axis, [(i, (i + 1) % count) for i in range(ends)])  31 us
    add x10, other arithmetic, relax(): centre + OMEGA * (source - (diagonal * centre - neighbours(padded))) / di...  22.4 us
    slice x19, local copies, waits for them, and re-layouts, with_halo(): head = lax.slice_in_dim(cells, 0, width, axis=dim)  16.1 us
  transfers between devices with their start and end apart: 78, of which 39 were waited for; matrix products, arithmetic and copies ran while one was open for 5% of the time, Pallas kernels for 0%

profile of v1, /device:TPU:1, one launch (start us, length us, event | category | flops | bytes accessed | tf_op | source)
XLA Modules:
  0.0 475.7 jit_solution(9090276044627978302)
XLA Ops:
  25.4 6.7 %collective-permute-start.5 = (f32[18,66,1]{1,0,2:T(8,128)}, f32[18,66,1]{1,0,2:T(8,128)}, u32[]{:S(2)}, u32[]{:S(2)}) collective-permute-start(f32[18,66,1]{1,0,2:T(8,128)} %copy.39), channel_id=1, source_target_pairs={{0,1},{2,3},{4,5},{6,7},{8,9},{10,11},{12,13},{14,15},{16,17},{18,... | collective-permute-start | bytes 14264 | tf_op jit(solution)/shard_map/ppermute | solution.py:23
  59.5 5.5 %collective-permute-start.11 = (f32[18,66,1]{1,0,2:T(8,128)S(1)}, f32[18,66,1]{1,0,2:T(8,128)S(1)}, u32[]{:S(2)}, u32[]{:S(2)}) collective-permute-start(f32[18,66,1]{1,0,2:T(8,128)S(1)} %copy.43), channel_id=1, source_target_pairs={{0,1},{2,3},{4,5},{6,7},{8,9},{10,11},{12,13},{14,15},{16,17},{18,... | collective-permute-start | bytes 14264 | tf_op jit(solution)/shard_map/ppermute | solution.py:23
  67.4 6.9 %fusion.35 = f32[16,64,256]{2,1,0:T(8,128)S(1)} fusion(f32[16,64,256]{2,1,0:T(8,128)} %copy-done.5, f32[16,64,256]{2,1,0:T(8,128)S(1)} %copy-done.2, f32[18,66,1]{2,1,0:T(8,128)} %copy.44, f32[18,1,256]{2,1,0:T(1,128)} %copy-done.23, f32[18,1,256]{2,1,0:T(1,128)} %copy-done.27, f32[1,64,256]{2,1,0:T(8,128)S(1)} %collective-permute-done.6, ...), kind=kLoop, calls=%fused_computation.99 | loop fusion | flops 7864320 | bytes 4371744 | tf_op jit(solution)/shard_map/add | solution.py:40
  83.5 5.8 %collective-permute-start.15 = (f32[18,1,256]{2,1,0:T(1,128)S(1)}, f32[18,1,256]{2,1,0:T(1,128)S(1)}, u32[]{:S(2)}, u32[]{:S(2)}) collective-permute-start(f32[18,1,256]{2,1,0:T(1,128)S(1)} %get-tuple-element.26), channel_id=1, source_target_pairs={{0,2},{2,4},{4,6},{6,8},{8,10},{10,12},{12,14},{14,16},{16,18},{18... | collective-permute-start | bytes 55304 | tf_op jit(solution)/shard_map/ppermute | solution.py:23
  96.4 7.2 %collective-permute-start.17 = (f32[18,66,1]{1,0,2:T(8,128)}, f32[18,66,1]{1,0,2:T(8,128)}, u32[]{:S(2)}, u32[]{:S(2)}) collective-permute-start(f32[18,66,1]{1,0,2:T(8,128)} %copy.47), channel_id=1, source_target_pairs={{0,1},{2,3},{4,5},{6,7},{8,9},{10,11},{12,13},{14,15},{16,17},{18,... | collective-permute-start | bytes 14264 | tf_op jit(solution)/shard_map/ppermute | solution.py:23
  133.2 6.4 %collective-permute-start.23 = (f32[18,66,1]{1,0,2:T(8,128)}, f32[18,66,1]{1,0,2:T(8,128)S(1)}, u32[]{:S(2)}, u32[]{:S(2)}) collective-permute-start(f32[18,66,1]{1,0,2:T(8,128)} %copy.51), channel_id=1, source_target_pairs={{0,1},{2,3},{4,5},{6,7},{8,9},{10,11},{12,13},{14,15},{16,17},{18,... | collective-permute-start | bytes 14264 | tf_op jit(solution)/shard_map/ppermute | solution.py:23
  144.5 6.9 %fusion.15 = f32[16,64,256]{2,1,0:T(8,128)S(1)} fusion(f32[16,64,256]{2,1,0:T(8,128)} %copy-done.4, f32[16,64,256]{2,1,0:T(8,128)S(1)} %copy-done.2, f32[18,66,1]{2,1,0:T(8,128)} %copy.52, f32[18,1,256]{2,1,0:T(1,128)} %copy-done.19, f32[18,1,256]{2,1,0:T(1,128)} %copy-done.24, f32[1,64,256]{2,1,0:T(8,128)S(1)} %copy-done.11, ...), kind=kLoop, calls=%fused_computation.43 | loop fusion | flops 7864320 | bytes 4371744 | tf_op jit(solution)/shard_map/add | solution.py:40
  160.7 6.0 %collective-permute-start.27 = (f32[18,1,256]{2,1,0:T(1,128)S(1)}, f32[18,1,256]{2,1,0:T(1,128)S(1)}, u32[]{:S(2)}, u32[]{:S(2)}) collective-permute-start(f32[18,1,256]{2,1,0:T(1,128)S(1)} %get-tuple-element.22), channel_id=1, source_target_pairs={{0,2},{2,4},{4,6},{6,8},{8,10},{10,12},{12,14},{14,16},{16,18},{18... | collective-permute-start | bytes 55304 | tf_op jit(solution)/shard_map/ppermute | solution.py:23
  174.4 6.7 %collective-permute-start.29 = (f32[18,66,1]{1,0,2:T(8,128)}, f32[18,66,1]{1,0,2:T(8,128)}, u32[]{:S(2)}, u32[]{:S(2)}) collective-permute-start(f32[18,66,1]{1,0,2:T(8,128)} %copy.55), channel_id=1, source_target_pairs={{0,1},{2,3},{4,5},{6,7},{8,9},{10,11},{12,13},{14,15},{16,17},{18,... | collective-permute-start | bytes 14264 | tf_op jit(solution)/shard_map/ppermute | solution.py:23
  200.7 5.6 %collective-permute-start.33 = (f32[10,1,128]{2,1,0:T(1,128)S(1)}, f32[10,1,128]{2,1,0:T(1,128)S(1)}, u32[]{:S(2)}, u32[]{:S(2)}) collective-permute-start(f32[10,1,128]{2,1,0:T(1,128)S(1)} %get-tuple-element.56), channel_id=1, source_target_pairs={{0,2},{2,4},{4,6},{6,8},{8,10},{10,12},{12,14},{14,16},{16,18},{18... | collective-permute-start | bytes 15368 | tf_op jit(solution)/shard_map/ppermute | solution.py:23
  208.5 5.5 %collective-permute-start.35 = (f32[10,34,1]{2,1,0:T(8,128)S(1)}, f32[10,34,1]{2,1,0:T(8,128)S(1)}, u32[]{:S(2)}, u32[]{:S(2)}) collective-permute-start(f32[10,34,1]{2,1,0:T(8,128)S(1)} %get-tuple-element.49), channel_id=1, source_target_pairs={{0,1},{2,3},{4,5},{6,7},{8,9},{10,11},{12,13},{14,15},{16,17},{18,... | collective-permute-start | bytes 4088 | tf_op jit(solution)/shard_map/ppermute | solution.py:23
  225.7 6.6 %collective-permute-start.39 = (f32[10,1,128]{2,1,0:T(1,128)S(1)}, f32[10,1,128]{2,1,0:T(1,128)S(1)}, u32[]{:S(2)}, u32[]{:S(2)}) collective-permute-start(f32[10,1,128]{2,1,0:T(1,128)S(1)} %get-tuple-element.54), channel_id=1, source_target_pairs={{0,2},{2,4},{4,6},{6,8},{8,10},{10,12},{12,14},{14,16},{16,18},{18... | collective-permute-start | bytes 15368 | tf_op jit(solution)/shard_map/ppermute | solution.py:23
  234.5 6.2 %collective-permute-start.41 = (f32[10,34,1]{2,1,0:T(8,128)S(1)}, f32[10,34,1]{2,1,0:T(8,128)S(1)}, u32[]{:S(2)}, u32[]{:S(2)}) collective-permute-start(f32[10,34,1]{2,1,0:T(8,128)S(1)} %get-tuple-element.47), channel_id=1, source_target_pairs={{0,1},{2,3},{4,5},{6,7},{8,9},{10,11},{12,13},{14,15},{16,17},{18,... | collective-permute-start | bytes 4088 | tf_op jit(solution)/shard_map/ppermute | solution.py:23
  259.9 6.2 %collective-permute-start.47 = (f32[10,34,1]{2,1,0:T(8,128)S(1)}, f32[10,34,1]{2,1,0:T(8,128)S(1)}, u32[]{:S(2)}, u32[]{:S(2)}) collective-permute-start(f32[10,34,1]{2,1,0:T(8,128)S(1)} %get-tuple-element.45), channel_id=1, source_target_pairs={{0,1},{2,3},{4,5},{6,7},{8,9},{10,11},{12,13},{14,15},{16,17},{18,... | collective-permute-start | bytes 4088 | tf_op jit(solution)/shard_map/ppermute | solution.py:23
  285.4 6.2 %collective-permute-start.53 = (f32[10,34,1]{2,1,0:T(8,128)S(1)}, f32[10,34,1]{2,1,0:T(8,128)S(1)}, u32[]{:S(2)}, u32[]{:S(2)}) collective-permute-start(f32[10,34,1]{2,1,0:T(8,128)S(1)} %get-tuple-element.43), channel_id=1, source_target_pairs={{0,1},{2,3},{4,5},{6,7},{8,9},{10,11},{12,13},{14,15},{16,17},{18,... | collective-permute-start | bytes 4088 | tf_op jit(solution)/shard_map/ppermute | solution.py:23
  303.6 5.4 %collective-permute-start.57 = (f32[6,1,64]{2,1,0:T(1,128)S(1)}, f32[6,1,64]{2,1,0:T(1,128)S(1)}, u32[]{:S(2)}, u32[]{:S(2)}) collective-permute-start(f32[6,1,64]{2,1,0:T(1,128)S(1)} %get-tuple-element.82), channel_id=1, source_target_pairs={{0,2},{2,4},{4,6},{6,8},{8,10},{10,12},{12,14},{14,16},{16,18},{18... | collective-permute-start | bytes 4616 | tf_op jit(solution)/shard_map/ppermute | solution.py:23
  311.2 6.2 %collective-permute-start.59 = (f32[6,18,1]{2,1,0:T(8,128)S(1)}, f32[6,18,1]{2,1,0:T(8,128)S(1)}, u32[]{:S(2)}, u32[]{:S(2)}) collective-permute-start(f32[6,18,1]{2,1,0:T(8,128)S(1)} %get-tuple-element.75), channel_id=1, source_target_pairs={{0,1},{2,3},{4,5},{6,7},{8,9},{10,11},{12,13},{14,15},{16,17},{18,... | collective-permute-start | bytes 1304 | tf_op jit(solution)/shard_map/ppermute | solution.py:23
  327.5 6.3 %collective-permute-start.63 = (f32[6,1,64]{2,1,0:T(1,128)S(1)}, f32[6,1,64]{2,1,0:T(1,128)S(1)}, u32[]{:S(2)}, u32[]{:S(2)}) collective-permute-start(f32[6,1,64]{2,1,0:T(1,128)S(1)} %get-tuple-element.80), channel_id=1, source_target_pairs={{0,2},{2,4},{4,6},{6,8},{8,10},{10,12},{12,14},{14,16},{16,18},{18... | collective-permute-start | bytes 4616 | tf_op jit(solution)/shard_map/ppermute | solution.py:23
  335.9 6.1 %collective-permute-start.65 = (f32[6,18,1]{2,1,0:T(8,128)S(1)}, f32[6,18,1]{2,1,0:T(8,128)S(1)}, u32[]{:S(2)}, u32[]{:S(2)}) collective-permute-start(f32[6,18,1]{2,1,0:T(8,128)S(1)} %get-tuple-element.73), channel_id=1, source_target_pairs={{0,1},{2,3},{4,5},{6,7},{8,9},{10,11},{12,13},{14,15},{16,17},{18,... | collective-permute-start | bytes 1304 | tf_op jit(solution)/shard_map/ppermute | solution.py:23
  352.1 6.5 %collective-permute-start.69 = (f32[6,1,64]{2,1,0:T(1,128)S(1)}, f32[6,1,64]{2,1,0:T(1,128)S(1)}, u32[]{:S(2)}, u32[]{:S(2)}) collective-permute-start(f32[6,1,64]{2,1,0:T(1,128)S(1)} %get-tuple-element.78), channel_id=1, source_target_pairs={{0,2},{2,4},{4,6},{6,8},{8,10},{10,12},{12,14},{14,16},{16,18},{18... | collective-permute-start | bytes 4616 | tf_op jit(solution)/shard_map/ppermute | solution.py:23
  360.7 6.1 %collective-permute-start.71 = (f32[6,18,1]{2,1,0:T(8,128)S(1)}, f32[6,18,1]{2,1,0:T(8,128)S(1)}, u32[]{:S(2)}, u32[]{:S(2)}) collective-permute-start(f32[6,18,1]{2,1,0:T(8,128)S(1)} %get-tuple-element.71), channel_id=1, source_target_pairs={{0,1},{2,3},{4,5},{6,7},{8,9},{10,11},{12,13},{14,15},{16,17},{18,... | collective-permute-start | bytes 1304 | tf_op jit(solution)/shard_map/ppermute | solution.py:23
  376.9 6.5 %collective-permute-start.75 = (f32[6,1,64]{2,1,0:T(1,128)S(1)}, f32[6,1,64]{2,1,0:T(1,128)S(1)}, u32[]{:S(2)}, u32[]{:S(2)}) collective-permute-start(f32[6,1,64]{2,1,0:T(1,128)S(1)} %get-tuple-element.76), channel_id=1, source_target_pairs={{0,2},{2,4},{4,6},{6,8},{8,10},{10,12},{12,14},{14,16},{16,18},{18... | collective-permute-start | bytes 4616 | tf_op jit(solution)/shard_map/ppermute | solution.py:23
  385.5 6.3 %collective-permute-start.77 = (f32[6,18,1]{2,1,0:T(8,128)S(1)}, f32[6,18,1]{2,1,0:T(8,128)S(1)}, u32[]{:S(2)}, u32[]{:S(2)}) collective-permute-start(f32[6,18,1]{2,1,0:T(8,128)S(1)} %get-tuple-element.69), channel_id=1, source_target_pairs={{0,1},{2,3},{4,5},{6,7},{8,9},{10,11},{12,13},{14,15},{16,17},{18,... | collective-permute-start | bytes 1304 | tf_op jit(solution)/shard_map/ppermute | solution.py:23
  398.5 76.4 %psum.7 = f32[1024]{0:T(1024)S(1)} all-reduce(f32[1024]{0:T(1024)S(1)} %bitcast.58), channel_id=1, replica_groups=mesh['gx'=4,'gy'=16,'gz'=2] {'gx','gy','gz'}, use_global_device_ids=true, to_apply=%region_0.1 | all-reduce | flops 1024 | bytes 8192 | tf_op jit(solution)/shard_map/psum | solution.py:105
  (308 shorter events, 253.3 us)
Async XLA Ops:
  22.0 10.0 %collective-permute-start.4 = (f32[18,66,1]{1,0,2:T(8,128)S(1)}, f32[18,66,1]{1,0,2:T(8,128)}, u32[]{:S(2)}, u32[]{:S(2)}) collective-permute-start(f32[18,66,1]{1,0,2:T(8,128)S(1)} %copy.37), channel_id=1, source_target_pairs={{1,0},{3,2},{5,4},{7,6},{9,8},{11,10},{13,12},{15,14},{17,16},{19,... | collective-permute-start | bytes 14264 | tf_op jit(solution)/shard_map/ppermute | solution.py:25
  25.4 8.5 %collective-permute-start.5 = (f32[18,66,1]{1,0,2:T(8,128)}, f32[18,66,1]{1,0,2:T(8,128)}, u32[]{:S(2)}, u32[]{:S(2)}) collective-permute-start(f32[18,66,1]{1,0,2:T(8,128)} %copy.39), channel_id=1, source_target_pairs={{0,1},{2,3},{4,5},{6,7},{8,9},{10,11},{12,13},{14,15},{16,17},{18,... | collective-permute-start | bytes 14264 | tf_op jit(solution)/shard_map/ppermute | solution.py:23
  81.6 7.8 %collective-permute-start.14 = (f32[18,1,256]{2,1,0:T(1,128)S(1)}, f32[18,1,256]{2,1,0:T(1,128)S(1)}, u32[]{:S(2)}, u32[]{:S(2)}) collective-permute-start(f32[18,1,256]{2,1,0:T(1,128)S(1)} %get-tuple-element.27), channel_id=1, source_target_pairs={{2,0},{4,2},{6,4},{8,6},{10,8},{12,10},{14,12},{16,14},{18,16},{20... | collective-permute-start | bytes 55304 | tf_op jit(solution)/shard_map/ppermute | solution.py:25
  93.1 11.4 %collective-permute-start.16 = (f32[18,66,1]{1,0,2:T(8,128)S(1)}, f32[18,66,1]{1,0,2:T(8,128)}, u32[]{:S(2)}, u32[]{:S(2)}) collective-permute-start(f32[18,66,1]{1,0,2:T(8,128)S(1)} %copy.45), channel_id=1, source_target_pairs={{1,0},{3,2},{5,4},{7,6},{9,8},{11,10},{13,12},{15,14},{17,16},{19,... | collective-permute-start | bytes 14264 | tf_op jit(solution)/shard_map/ppermute | solution.py:25
  96.4 9.9 %collective-permute-start.17 = (f32[18,66,1]{1,0,2:T(8,128)}, f32[18,66,1]{1,0,2:T(8,128)}, u32[]{:S(2)}, u32[]{:S(2)}) collective-permute-start(f32[18,66,1]{1,0,2:T(8,128)} %copy.47), channel_id=1, source_target_pairs={{0,1},{2,3},{4,5},{6,7},{8,9},{10,11},{12,13},{14,15},{16,17},{18,... | collective-permute-start | bytes 14264 | tf_op jit(solution)/shard_map/ppermute | solution.py:23
  131.0 10.5 %collective-permute-start.22 = (f32[18,66,1]{1,0,2:T(8,128)}, f32[18,66,1]{1,0,2:T(8,128)}, u32[]{:S(2)}, u32[]{:S(2)}) collective-permute-start(f32[18,66,1]{1,0,2:T(8,128)} %copy.49), channel_id=1, source_target_pairs={{1,0},{3,2},{5,4},{7,6},{9,8},{11,10},{13,12},{15,14},{17,16},{19,... | collective-permute-start | bytes 14264 | tf_op jit(solution)/shard_map/ppermute | solution.py:25
  133.2 10.1 %collective-permute-start.23 = (f32[18,66,1]{1,0,2:T(8,128)}, f32[18,66,1]{1,0,2:T(8,128)S(1)}, u32[]{:S(2)}, u32[]{:S(2)}) collective-permute-start(f32[18,66,1]{1,0,2:T(8,128)} %copy.51), channel_id=1, source_target_pairs={{0,1},{2,3},{4,5},{6,7},{8,9},{10,11},{12,13},{14,15},{16,17},{18,... | collective-permute-start | bytes 14264 | tf_op jit(solution)/shard_map/ppermute | solution.py:23
  158.8 8.5 %collective-permute-start.26 = (f32[18,1,256]{2,1,0:T(1,128)S(1)}, f32[18,1,256]{2,1,0:T(1,128)S(1)}, u32[]{:S(2)}, u32[]{:S(2)}) collective-permute-start(f32[18,1,256]{2,1,0:T(1,128)S(1)} %get-tuple-element.23), channel_id=1, source_target_pairs={{2,0},{4,2},{6,4},{8,6},{10,8},{12,10},{14,12},{16,14},{18,16},{20... | collective-permute-start | bytes 55304 | tf_op jit(solution)/shard_map/ppermute | solution.py:25
  171.1 12.0 %collective-permute-start.28 = (f32[18,66,1]{1,0,2:T(8,128)}, f32[18,66,1]{1,0,2:T(8,128)}, u32[]{:S(2)}, u32[]{:S(2)}) collective-permute-start(f32[18,66,1]{1,0,2:T(8,128)} %copy.53), channel_id=1, source_target_pairs={{1,0},{3,2},{5,4},{7,6},{9,8},{11,10},{13,12},{15,14},{17,16},{19,... | collective-permute-start | bytes 14264 | tf_op jit(solution)/shard_map/ppermute | solution.py:25
  174.4 10.6 %collective-permute-start.29 = (f32[18,66,1]{1,0,2:T(8,128)}, f32[18,66,1]{1,0,2:T(8,128)}, u32[]{:S(2)}, u32[]{:S(2)}) collective-permute-start(f32[18,66,1]{1,0,2:T(8,128)} %copy.55), channel_id=1, source_target_pairs={{0,1},{2,3},{4,5},{6,7},{8,9},{10,11},{12,13},{14,15},{16,17},{18,... | collective-permute-start | bytes 14264 | tf_op jit(solution)/shard_map/ppermute | solution.py:23
  207.2 8.0 %collective-permute-start.34 = (f32[10,34,1]{2,1,0:T(8,128)S(1)}, f32[10,34,1]{2,1,0:T(8,128)S(1)}, u32[]{:S(2)}, u32[]{:S(2)}) collective-permute-start(f32[10,34,1]{2,1,0:T(8,128)S(1)} %get-tuple-element.48), channel_id=1, source_target_pairs={{1,0},{3,2},{5,4},{7,6},{9,8},{11,10},{13,12},{15,14},{17,16},{19,... | collective-permute-start | bytes 4088 | tf_op jit(solution)/shard_map/ppermute | solution.py:25
  208.5 8.2 %collective-permute-start.35 = (f32[10,34,1]{2,1,0:T(8,128)S(1)}, f32[10,34,1]{2,1,0:T(8,128)S(1)}, u32[]{:S(2)}, u32[]{:S(2)}) collective-permute-start(f32[10,34,1]{2,1,0:T(8,128)S(1)} %get-tuple-element.49), channel_id=1, source_target_pairs={{0,1},{2,3},{4,5},{6,7},{8,9},{10,11},{12,13},{14,15},{16,17},{18,... | collective-permute-start | bytes 4088 | tf_op jit(solution)/shard_map/ppermute | solution.py:23
  223.8 8.5 %collective-permute-start.38 = (f32[10,1,128]{2,1,0:T(1,128)S(1)}, f32[10,1,128]{2,1,0:T(1,128)S(1)}, u32[]{:S(2)}, u32[]{:S(2)}) collective-permute-start(f32[10,1,128]{2,1,0:T(1,128)S(1)} %get-tuple-element.55), channel_id=1, source_target_pairs={{2,0},{4,2},{6,4},{8,6},{10,8},{12,10},{14,12},{16,14},{18,16},{20... | collective-permute-start | bytes 15368 | tf_op jit(solution)/shard_map/ppermute | solution.py:25
  233.2 8.7 %collective-permute-start.40 = (f32[10,34,1]{2,1,0:T(8,128)S(1)}, f32[10,34,1]{2,1,0:T(8,128)S(1)}, u32[]{:S(2)}, u32[]{:S(2)}) collective-permute-start(f32[10,34,1]{2,1,0:T(8,128)S(1)} %get-tuple-element.46), channel_id=1, source_target_pairs={{1,0},{3,2},{5,4},{7,6},{9,8},{11,10},{13,12},{15,14},{17,16},{19,... | collective-permute-start | bytes 4088 | tf_op jit(solution)/shard_map/ppermute | solution.py:25
  234.5 8.9 %collective-permute-start.41 = (f32[10,34,1]{2,1,0:T(8,128)S(1)}, f32[10,34,1]{2,1,0:T(8,128)S(1)}, u32[]{:S(2)}, u32[]{:S(2)}) collective-permute-start(f32[10,34,1]{2,1,0:T(8,128)S(1)} %get-tuple-element.47), channel_id=1, source_target_pairs={{0,1},{2,3},{4,5},{6,7},{8,9},{10,11},{12,13},{14,15},{16,17},{18,... | collective-permute-start | bytes 4088 | tf_op jit(solution)/shard_map/ppermute | solution.py:23
  258.6 8.8 %collective-permute-start.46 = (f32[10,34,1]{2,1,0:T(8,128)S(1)}, f32[10,34,1]{2,1,0:T(8,128)S(1)}, u32[]{:S(2)}, u32[]{:S(2)}) collective-permute-start(f32[10,34,1]{2,1,0:T(8,128)S(1)} %get-tuple-element.44), channel_id=1, source_target_pairs={{1,0},{3,2},{5,4},{7,6},{9,8},{11,10},{13,12},{15,14},{17,16},{19,... | collective-permute-start | bytes 4088 | tf_op jit(solution)/shard_map/ppermute | solution.py:25
  259.9 8.9 %collective-permute-start.47 = (f32[10,34,1]{2,1,0:T(8,128)S(1)}, f32[10,34,1]{2,1,0:T(8,128)S(1)}, u32[]{:S(2)}, u32[]{:S(2)}) collective-permute-start(f32[10,34,1]{2,1,0:T(8,128)S(1)} %get-tuple-element.45), channel_id=1, source_target_pairs={{0,1},{2,3},{4,5},{6,7},{8,9},{10,11},{12,13},{14,15},{16,17},{18,... | collective-permute-start | bytes 4088 | tf_op jit(solution)/shard_map/ppermute | solution.py:23
  284.1 8.8 %collective-permute-start.52 = (f32[10,34,1]{2,1,0:T(8,128)S(1)}, f32[10,34,1]{2,1,0:T(8,128)S(1)}, u32[]{:S(2)}, u32[]{:S(2)}) collective-permute-start(f32[10,34,1]{2,1,0:T(8,128)S(1)} %get-tuple-element.42), channel_id=1, source_target_pairs={{1,0},{3,2},{5,4},{7,6},{9,8},{11,10},{13,12},{15,14},{17,16},{19,... | collective-permute-start | bytes 4088 | tf_op jit(solution)/shard_map/ppermute | solution.py:25
  285.4 8.9 %collective-permute-start.53 = (f32[10,34,1]{2,1,0:T(8,128)S(1)}, f32[10,34,1]{2,1,0:T(8,128)S(1)}, u32[]{:S(2)}, u32[]{:S(2)}) collective-permute-start(f32[10,34,1]{2,1,0:T(8,128)S(1)} %get-tuple-element.43), channel_id=1, source_target_pairs={{0,1},{2,3},{4,5},{6,7},{8,9},{10,11},{12,13},{14,15},{16,17},{18,... | collective-permute-start | bytes 4088 | tf_op jit(solution)/shard_map/ppermute | solution.py:23
  311.2 7.6 %collective-permute-start.59 = (f32[6,18,1]{2,1,0:T(8,128)S(1)}, f32[6,18,1]{2,1,0:T(8,128)S(1)}, u32[]{:S(2)}, u32[]{:S(2)}) collective-permute-start(f32[6,18,1]{2,1,0:T(8,128)S(1)} %get-tuple-element.75), channel_id=1, source_target_pairs={{0,1},{2,3},{4,5},{6,7},{8,9},{10,11},{12,13},{14,15},{16,17},{18,... | collective-permute-start | bytes 1304 | tf_op jit(solution)/shard_map/ppermute | solution.py:23
  325.5 8.3 %collective-permute-start.62 = (f32[6,1,64]{2,1,0:T(1,128)S(1)}, f32[6,1,64]{2,1,0:T(1,128)S(1)}, u32[]{:S(2)}, u32[]{:S(2)}) collective-permute-start(f32[6,1,64]{2,1,0:T(1,128)S(1)} %get-tuple-element.81), channel_id=1, source_target_pairs={{2,0},{4,2},{6,4},{8,6},{10,8},{12,10},{14,12},{16,14},{18,16},{20... | collective-permute-start | bytes 4616 | tf_op jit(solution)/shard_map/ppermute | solution.py:25
  350.2 8.4 %collective-permute-start.68 = (f32[6,1,64]{2,1,0:T(1,128)S(1)}, f32[6,1,64]{2,1,0:T(1,128)S(1)}, u32[]{:S(2)}, u32[]{:S(2)}) collective-permute-start(f32[6,1,64]{2,1,0:T(1,128)S(1)} %get-tuple-element.79), channel_id=1, source_target_pairs={{2,0},{4,2},{6,4},{8,6},{10,8},{12,10},{14,12},{16,14},{18,16},{20... | collective-permute-start | bytes 4616 | tf_op jit(solution)/shard_map/ppermute | solution.py:25
  375.0 8.4 %collective-permute-start.74 = (f32[6,1,64]{2,1,0:T(1,128)S(1)}, f32[6,1,64]{2,1,0:T(1,128)S(1)}, u32[]{:S(2)}, u32[]{:S(2)}) collective-permute-start(f32[6,1,64]{2,1,0:T(1,128)S(1)} %get-tuple-element.77), channel_id=1, source_target_pairs={{2,0},{4,2},{6,4},{8,6},{10,8},{12,10},{14,12},{16,14},{18,16},{20... | collective-permute-start | bytes 4616 | tf_op jit(solution)/shard_map/ppermute | solution.py:25
  384.2 7.7 %collective-permute-start.76 = (f32[6,18,1]{2,1,0:T(8,128)S(1)}, f32[6,18,1]{2,1,0:T(8,128)S(1)}, u32[]{:S(2)}, u32[]{:S(2)}) collective-permute-start(f32[6,18,1]{2,1,0:T(8,128)S(1)} %get-tuple-element.68), channel_id=1, source_target_pairs={{1,0},{3,2},{5,4},{7,6},{9,8},{11,10},{13,12},{15,14},{17,16},{19,... | collective-permute-start | bytes 1304 | tf_op jit(solution)/shard_map/ppermute | solution.py:25
  (85 other events, 1187.0 us)

commit v2 on v1

--- a/solution.py
+++ b/solution.py
@@ -63,38 +63,71 @@
     return flat.reshape(extent_a // 2, extent_b // 2, extent_c // 2) * 0.125
 
 
-def fine_rim(field):
-    return with_halo(field, (("gx", 0), ("gy", 1), ("gz", 2)), 1)
+def exchange(stack, width):
+    for axis, dim in (("gz", 3), ("gy", 2), ("gx", 1)):
+        count = lax.axis_size(axis)
+        head = lax.slice_in_dim(stack, 0, width, axis=dim)
+        tail = lax.slice_in_dim(stack, stack.shape[dim] - width, stack.shape[dim], axis=dim)
+        stack = jnp.concatenate(
+            [
+                lax.ppermute(tail, axis, [(i, i + 1) for i in range(count - 1)]),
+                stack,
+                lax.ppermute(head, axis, [(i + 1, i) for i in range(count - 1)]),
+            ],
+            axis=dim,
+        )
+    return stack
 
 
-def middle_rim(field):
-    return with_halo(field, (("gx", 0), ("gy", 1), ("gz", 2)), 1)
+def inside(shape, width):
+    masks = []
+    for axis, extent in zip(("gx", "gy", "gz"), shape):
+        place = lax.axis_index(axis) * extent - width
+        place = place + lax.broadcasted_iota(jnp.int32, (extent + 2 * width,), 0)
+        masks.append((place >= 0) & (place < extent * lax.axis_size(axis)))
+    return masks[0][:, None, None] & masks[1][None, :, None] & masks[2][None, None, :]
 
 
-def coarse_rim(field):
-    return with_halo(field, (("gx", 0), ("gy", 1), ("gz", 2)), 1)
+def crop(field, k):
+    if k == 0:
+        return field
+    return field[k:-k, k:-k, k:-k]
+
+
+def smooth_wide(start, source, diagonal, mask, steps):
+    current = start
+    for step in range(1, steps + 1):
+        current = relax(current, crop(source, step), crop(diagonal, step))
+        current = jnp.where(crop(mask, step), current, 0.0)
+    return current
+
+
+def coarser_level(source, damp):
+    width = SWEEPS
+    wide = exchange(jnp.stack([source, damp]), width)
+    wide_source = wide[0]
+    wide_diag = 6.0 + wide[1]
+    mask = inside(source.shape, width)
+    start = jnp.where(mask, OMEGA * wide_source / wide_diag, 0.0)
+    current = smooth_wide(start, wide_source, wide_diag, mask, SWEEPS - 1)
+    return crop(current, 1), defect(current, source, 6.0 + damp)
 
 
 def shards(right_side, initial_guess, damping, group_map, block_inverse):
-    fine_diag = 6.0 + damping
-    iterate = initial_guess
-    for sweep_count in range(SWEEPS):
-        iterate = relax(fine_rim(iterate), right_side, fine_diag)
-    fine_defect = defect(fine_rim(iterate), right_side, fine_diag)
+    width = SWEEPS + 1
+    wide = exchange(jnp.stack([initial_guess, right_side, damping]), width)
+    wide_source = wide[1]
+    wide_diag = 6.0 + wide[2]
+    mask = inside(right_side.shape, width)
+    current = smooth_wide(wide[0], wide_source, wide_diag, mask, SWEEPS)
+    iterate = crop(current, 1)
+    fine_defect = defect(current, right_side, 6.0 + damping)
     middle_damp = 4.0 * shrink(damping)
     middle_source = 4.0 * shrink(fine_defect)
-    middle_diag = 6.0 + middle_damp
-    middle = OMEGA * middle_source / middle_diag
-    for sweep_count in range(SWEEPS - 1):
-        middle = relax(middle_rim(middle), middle_source, middle_diag)
-    middle_defect = defect(middle_rim(middle), middle_source, middle_diag)
+    middle, middle_defect = coarser_level(middle_source, middle_damp)
     coarse_damp = 4.0 * shrink(middle_damp)
     coarse_source = 4.0 * shrink(middle_defect)
-    coarse_diag = 6.0 + coarse_damp
-    coarse = OMEGA * coarse_source / coarse_diag
-    for sweep_count in range(SWEEPS - 1):
-        coarse = relax(coarse_rim(coarse), coarse_source, coarse_diag)
-    coarse_defect = defect(coarse_rim(coarse), coarse_source, coarse_diag)
+    coarse, coarse_defect = coarser_level(coarse_source, coarse_damp)
     cells = coarse_defect.size
     one_hot = (
         group_map.reshape(cells, 1) == lax.broadcasted_iota(jnp.int32, (cells, NAGG), 1)

time: 479 us -> 293 us (0.61)
  starting transfers between devices: 274 us -> 53.3 us
  other arithmetic: 29.4 us -> 68.8 us
  waiting for transfers between devices: 38.2 us -> 68 us
  local copies, waits for them, and re-layouts: 43.5 us -> 15.1 us
  blocking collectives: 76.4 us -> 67.2 us
    ppermute x78 -> x18, starting transfers between devices: 274 us -> 53.3 us  [the longest x9 39.4 us: exchange(): lax.ppermute(tail, axis, [(i, i + 1) for i in range(count - 1)])]
    select_n x0 -> x12, other arithmetic: none -> 30.2 us  [the longest x10 29.9 us: smooth_wide(): current = jnp.where(crop(mask, step), current, 0.0)]
    ppermute x78 -> x18, waiting for transfers between devices: 38.2 us -> 68 us  [the longest x9 34.5 us: exchange(): lax.ppermute(head, axis, [(i + 1, i) for i in range(count - 1)])]
    add x10 -> x3, other arithmetic: 22.4 us -> 4.63 us  [the longest x1 4.52 us: shards(): wide_diag = 6.0 + wide[2]]
    slice x37 -> x6, local copies, waits for them, and re-layouts: 23.6 us -> 6.65 us  [the longest x4 4.65 us: exchange(): lax.slice_in_dim(stack, stack.shape[dim] - width, stack.shape[dim], axis=...]
    concatenate x25 -> x5, other arithmetic: 1.12 us -> 12.1 us  [exchange(): jnp.concatenate([lax.ppermute(tail, axis, [(i, i + 1) for i in range(coun...]
    psum x1, blocking collectives: 76.4 us -> 67.2 us  [shards(): summed = lax.psum(partial_sums, ('gx', 'gy', 'gz'))]
    ppermute x10 -> x4, local copies, waits for them, and re-layouts: 16.6 us -> 7.5 us  [the longest x2 3.76 us: exchange(): lax.ppermute(tail, axis, [(i, i + 1) for i in range(count - 1)])]
  transfers between devices with their start and end apart: 78 -> 18, of which waited for: 39 -> 12; matrix products, arithmetic and copies ran while one was open for 5% -> 7% of each run, Pallas kernels for 0% -> 0%
where the time goes in v2:
time: 293 us; the launch traced here: 288 us
  other arithmetic  68.8 us (23%)
  waiting for transfers between devices  68 us (23%)
  blocking collectives  67.2 us (23%)
  starting transfers between devices  53.3 us (18%)
  local copies, waits for them, and re-layouts  15.1 us (5%)
  matrix products  13.6 us (5%)
    psum x1, blocking collectives, shards(): summed = lax.psum(partial_sums, ('gx', 'gy', 'gz'))  67.2 us
    ppermute x9, starting transfers between devices, exchange(): lax.ppermute(tail, axis, [(i, i + 1) for i in range(count - 1)])  39.4 us
    ppermute x9, waiting for transfers between devices, exchange(): lax.ppermute(head, axis, [(i + 1, i) for i in range(count - 1)])  34.5 us
    ppermute x9, waiting for transfers between devices, exchange(): lax.ppermute(tail, axis, [(i, i + 1) for i in range(count - 1)])  33.5 us
    select_n x10, other arithmetic, smooth_wide(): current = jnp.where(crop(mask, step), current, 0.0)  29.9 us
    ppermute x9, starting transfers between devices, exchange(): lax.ppermute(head, axis, [(i + 1, i) for i in range(count - 1)])  13.9 us
    concatenate x5, other arithmetic, exchange(): jnp.concatenate([lax.ppermute(tail, axis, [(i, i + 1) for i in range(coun...  12.1 us
    slice x4, other arithmetic, exchange(): lax.slice_in_dim(stack, stack.shape[dim] - width, stack.shape[dim], axis=...  6.49 us
  transfers between devices with their start and end apart: 18, of which 12 were waited for; matrix products, arithmetic and copies ran while one was open for 7% of the time, Pallas kernels for 0%

profile of v2, /device:TPU:1, one launch (start us, length us, event | category | flops | bytes accessed | tf_op | source)
XLA Modules:
  0.0 287.8 jit_solution(12032623415496866514)
XLA Ops:
  6.7 6.3 %collective-permute-start = (f32[3,16,64,5]{2,1,3,0:T(8,128)S(1)}, f32[3,16,64,5]{2,1,3,0:T(8,128)}, u32[]{:S(2)}, u32[]{:S(2)}) collective-permute-start(f32[3,16,64,5]{2,1,3,0:T(8,128)S(1)} %copy.29), channel_id=1, source_target_pairs={{0,1},{2,3},{4,5},{6,7},{8,9},{10,11},{12,13},{14,15},{16,17},{18,... | collective-permute-start | bytes 184328 | tf_op jit(solution)/shard_map/ppermute | solution.py:73
  37.7 3.2 %collective-permute-done.3 = f32[3,16,5,266]{3,1,2,0:T(8,128)} collective-permute-done((f32[3,16,5,266]{3,1,2,0:T(8,128)}, f32[3,16,5,266]{3,1,2,0:T(8,128)}, u32[]{:S(2)}, u32[]{:S(2)}) %collective-permute-start.3) | collective-permute-done | bytes 255392 | tf_op jit(solution)/shard_map/ppermute | solution.py:75
  42.1 4.5 %pad_maximum_fusion.8 = (f32[3,5,74,266]{3,2,1,0:T(8,128)}, f32[3,5,74,266]{3,2,1,0:T(8,128)}) fusion(f32[3,16,5,266]{3,2,1,0:T(8,128)S(1)} %copy.36, f32[3,16,5,266]{3,2,1,0:T(8,128)S(1)} %copy.35, f32[3,16,64,5]{3,2,1,0:T(8,128)} %copy.32, f32[3,16,64,5]{3,2,1,0:T(8,128)S(1)} %copy-done.3, f32[1,16,64,256]{3,2,1,0:T(8,128)S(1)} %bitcast.59, ...), kind=kLoop, calls=%fused_computation.59 | loop fusion | flops 3543120 | bytes 6141408 | tf_op jit(solution)/shard_map/slice | solution.py:70
  46.7 4.8 %collective-permute-start.4 = (f32[3,5,74,266]{3,2,1,0:T(8,128)}, f32[3,5,74,266]{3,2,1,0:T(8,128)}, u32[]{:S(2)}, u32[]{:S(2)}) collective-permute-start(f32[3,5,74,266]{3,2,1,0:T(8,128)} %get-tuple-element.21), channel_id=1, source_target_pairs={{0,32},{32,64},{64,96},{1,33},{33,65},{65,97},{2,34},{34,66},{66,9... | collective-permute-start | bytes 3543128 | tf_op jit(solution)/shard_map/ppermute | solution.py:73
  59.9 27.4 %collective-permute-done.4 = f32[3,5,74,266]{3,2,1,0:T(8,128)} collective-permute-done((f32[3,5,74,266]{3,2,1,0:T(8,128)}, f32[3,5,74,266]{3,2,1,0:T(8,128)}, u32[]{:S(2)}, u32[]{:S(2)}) %collective-permute-start.4) | collective-permute-done | bytes 1181072 | tf_op jit(solution)/shard_map/ppermute | solution.py:73
  87.3 5.4 %collective-permute-done.5 = f32[3,5,74,266]{3,2,1,0:T(8,128)} collective-permute-done((f32[3,5,74,266]{3,2,1,0:T(8,128)}, f32[3,5,74,266]{3,2,1,0:T(8,128)}, u32[]{:S(2)}, u32[]{:S(2)}) %collective-permute-start.5) | collective-permute-done | bytes 1181072 | tf_op jit(solution)/shard_map/ppermute | solution.py:75
  92.7 11.2 %pad_maximum_fusion = f32[3,26,74,266]{3,2,1,0:T(8,128)} fusion(f32[3,5,74,266]{3,2,1,0:T(8,128)} %collective-permute-done.5, f32[3,16,5,266]{3,2,1,0:T(8,128)} %copy-done.7, f32[3,16,64,5]{3,2,1,0:T(8,128)} %copy.32, f32[1,16,64,256]{3,2,1,0:T(8,128)S(1)} %bitcast.60, f32[1,16,64,256]{3,2,1,0:T(8,128)S(1)} %bitcast.64, f32[1,16,64,256]{3,2,1,0:T(8,128)S(1)} %bitcast.68, ...), kind=kLoop, calls=%fused_computation.2 | loop fusion | flops 12282816 | bytes 12282816 | tf_op jit(solution)/shard_map/concatenate | solution.py:71
  103.9 4.5 %fusion.2 = (f32[26,74,266]{2,1,0:T(8,128)S(1)}, f32[26,74,266]{2,1,0:T(8,128)S(1)}, f32[26,74,266]{2,1,0:T(8,128)S(1)}) fusion(f32[3,26,74,266]{3,2,1,0:T(8,128)} %pad_maximum_fusion), kind=kLoop, calls=%fused_computation.5 | loop fusion | flops 511784 | bytes 12282816 | tf_op jit(solution)/shard_map/add | solution.py:120
  108.5 7.2 %fusion.8 = f32[24,72,264]{2,1,0:T(8,128)S(1)} fusion(f32[26,74,266]{2,1,0:T(8,128)S(1)} %get-tuple-element.20, f32[26,74,266]{2,1,0:T(8,128)S(1)} %get-tuple-element.19, f32[26,74,266]{2,1,0:T(8,128)S(1)} %get-tuple-element.18, pred[26,74,266]{2,1,0:T(8,128)(4,1)S(1)} %broadcast_and_fusion), kind=kLoop, calls=%fused_computation.15 | loop fusion | flops 5474304 | bytes 18703872 | tf_op jit(solution)/shard_map/jit(_where)/select_n | solution.py:101
  115.7 6.5 %fusion.14 = f32[22,70,262]{2,1,0:T(8,128)S(1)} fusion(f32[24,72,264]{2,1,0:T(8,128)S(1)} %fusion.8, f32[26,74,266]{2,1,0:T(8,128)S(1)} %get-tuple-element.19, f32[26,74,266]{2,1,0:T(8,128)S(1)} %get-tuple-element.18, pred[26,74,266]{2,1,0:T(8,128)(4,1)S(1)} %broadcast_and_fusion), kind=kLoop, calls=%fused_computation.26 | loop fusion | flops 4841760 | bytes 16542680 | tf_op jit(solution)/shard_map/jit(_where)/select_n | solution.py:101
  122.2 6.2 %fusion.20 = f32[20,68,260]{2,1,0:T(8,128)S(1)} fusion(f32[22,70,262]{2,1,0:T(8,128)S(1)} %fusion.14, f32[26,74,266]{2,1,0:T(8,128)S(1)} %get-tuple-element.19, f32[26,74,266]{2,1,0:T(8,128)S(1)} %get-tuple-element.18, pred[26,74,266]{2,1,0:T(8,128)(4,1)S(1)} %broadcast_and_fusion), kind=kLoop, calls=%fused_computation.37 | loop fusion | flops 4243200 | bytes 14497600 | tf_op jit(solution)/shard_map/jit(_where)/select_n | solution.py:101
  128.4 5.4 %fusion.26 = f32[18,66,258]{2,1,0:T(8,128)S(1)} fusion(f32[20,68,260]{2,1,0:T(8,128)S(1)} %fusion.20, f32[26,74,266]{2,1,0:T(8,128)S(1)} %get-tuple-element.19, f32[26,74,266]{2,1,0:T(8,128)S(1)} %get-tuple-element.18, pred[26,74,266]{2,1,0:T(8,128)(4,1)S(1)} %broadcast_and_fusion), kind=kLoop, calls=%fused_computation.48 | loop fusion | flops 3678048 | bytes 12566664 | tf_op jit(solution)/shard_map/jit(_where)/select_n | solution.py:101
  137.8 6.3 %collective-permute-start.6 = (f32[2,8,32,4]{3,2,1,0:T(8,128)S(1)}, f32[2,8,32,4]{3,2,1,0:T(8,128)S(1)}, u32[]{:S(2)}, u32[]{:S(2)}) collective-permute-start(f32[2,8,32,4]{3,2,1,0:T(8,128)S(1)} %get-tuple-element.35), channel_id=1, source_target_pairs={{0,1},{2,3},{4,5},{6,7},{8,9},{10,11},{12,13},{14,15},{16,17},{18,... | collective-permute-start | bytes 24584 | tf_op jit(solution)/shard_map/ppermute | solution.py:73
  147.7 5.6 %collective-permute-done.7 = f32[2,8,32,4]{3,2,1,0:T(8,128)S(1)} collective-permute-done((f32[2,8,32,4]{3,2,1,0:T(8,128)S(1)}, f32[2,8,32,4]{3,2,1,0:T(8,128)S(1)}, u32[]{:S(2)}, u32[]{:S(2)}) %collective-permute-start.7) | collective-permute-done | bytes 8224 | tf_op jit(solution)/shard_map/ppermute | solution.py:75
  153.4 8.1 %collective-permute-start.8 = (f32[2,8,4,136]{3,2,1,0:T(4,128)S(1)}, f32[2,8,4,136]{3,2,1,0:T(4,128)S(1)}, u32[]{:S(2)}, u32[]{:S(2)}) collective-permute-start(f32[2,8,4,136]{3,2,1,0:T(4,128)S(1)} %get-tuple-element.29), channel_id=1, source_target_pairs={{0,2},{2,4},{4,6},{6,8},{8,10},{10,12},{12,14},{14,16},{16,18},{18... | collective-permute-start | bytes 104456 | tf_op jit(solution)/shard_map/ppermute | solution.py:73
  163.5 3.6 %collective-permute-done.9 = f32[2,8,4,136]{3,2,1,0:T(4,128)S(1)} collective-permute-done((f32[2,8,4,136]{3,2,1,0:T(4,128)S(1)}, f32[2,8,4,136]{3,2,1,0:T(4,128)S(1)}, u32[]{:S(2)}, u32[]{:S(2)}) %collective-permute-start.9) | collective-permute-done | bytes 34848 | tf_op jit(solution)/shard_map/ppermute | solution.py:75
  171.7 3.6 %collective-permute-done.10 = f32[2,4,40,136]{3,2,1,0:T(8,128)S(1)} collective-permute-done((f32[2,4,40,136]{3,2,1,0:T(8,128)S(1)}, f32[2,4,40,136]{3,2,1,0:T(8,128)S(1)}, u32[]{:S(2)}, u32[]{:S(2)}) %collective-permute-start.10) | collective-permute-done | bytes 174112 | tf_op jit(solution)/shard_map/ppermute | solution.py:73
  175.3 4.1 %collective-permute-done.11 = f32[2,4,40,136]{3,2,1,0:T(8,128)S(1)} collective-permute-done((f32[2,4,40,136]{3,2,1,0:T(8,128)S(1)}, f32[2,4,40,136]{3,2,1,0:T(8,128)S(1)}, u32[]{:S(2)}, u32[]{:S(2)}) %collective-permute-start.11) | collective-permute-done | bytes 174112 | tf_op jit(solution)/shard_map/ppermute | solution.py:75
  189.0 5.6 %collective-permute-done.13 = f32[2,4,16,4]{3,2,1,0:T(8,128)S(1)} collective-permute-done((f32[2,4,16,4]{3,2,1,0:T(8,128)S(1)}, f32[2,4,16,4]{3,2,1,0:T(8,128)S(1)}, u32[]{:S(2)}, u32[]{:S(2)}) %collective-permute-start.13) | collective-permute-done | bytes 2080 | tf_op jit(solution)/shard_map/ppermute | solution.py:75
  194.8 3.5 %collective-permute-start.14 = (f32[2,4,4,72]{3,2,1,0:T(4,128)S(1)}, f32[2,4,4,72]{3,2,1,0:T(4,128)S(1)}, u32[]{:S(2)}, u32[]{:S(2)}) collective-permute-start(f32[2,4,4,72]{3,2,1,0:T(4,128)S(1)} %get-tuple-element.37), channel_id=1, source_target_pairs={{0,2},{2,4},{4,6},{6,8},{8,10},{10,12},{12,14},{14,16},{16,18},{18... | collective-permute-start | bytes 27656 | tf_op jit(solution)/shard_map/ppermute | solution.py:73
  203.5 3.2 %collective-permute-start.16 = (f32[2,4,24,72]{3,2,1,0:T(8,128)S(1)}, f32[2,4,24,72]{3,2,1,0:T(8,128)S(1)}, u32[]{:S(2)}, u32[]{:S(2)}) collective-permute-start(f32[2,4,24,72]{3,2,1,0:T(8,128)S(1)} %pad_maximum_fusion.18), channel_id=1, source_target_pairs={{0,32},{32,64},{64,96},{1,33},{33,65},{65,97},{2,34},{34,66},{66,9... | collective-permute-start | bytes 165896 | tf_op jit(solution)/shard_map/ppermute | solution.py:73
  208.3 3.7 %collective-permute-done.17 = f32[2,4,24,72]{3,2,1,0:T(8,128)S(1)} collective-permute-done((f32[2,4,24,72]{3,2,1,0:T(8,128)S(1)}, f32[2,4,24,72]{3,2,1,0:T(8,128)S(1)}, u32[]{:S(2)}, u32[]{:S(2)}) %collective-permute-start.17) | collective-permute-done | bytes 55328 | tf_op jit(solution)/shard_map/ppermute | solution.py:75
  214.1 5.3 %fusion = f32[1,1024]{1,0:T(1,128)S(1)} fusion(f32[4096,1]{0,1:T(1,128)S(1)} %reshape.280, s32[4096]{0:T(1024)S(1)} %eq.38), kind=kOutput, calls=%fused_computation.1 | convolution fusion | flops 54525952 | bytes 36864 | tf_op jit(solution)/shard_map/dot_general | solution.py:135
  219.4 67.2 %psum.7 = f32[1024]{0:T(1024)S(1)} all-reduce(f32[1024]{0:T(1024)S(1)} %bitcast.97), channel_id=1, replica_groups=mesh['gx'=4,'gy'=16,'gz'=2] {'gx','gy','gz'}, use_global_device_ids=true, to_apply=%region_0.1 | all-reduce | flops 1024 | bytes 8192 | tf_op jit(solution)/shard_map/psum | solution.py:138
  (133 shorter events, 73.3 us)
Async XLA Ops:
  0.6 285.9 %copy-start = (f32[64,1024]{1,0:T(8,128)S(1)}, f32[64,1024]{1,0:T(8,128)}, u32[]{:S(2)}) copy-start(f32[64,1024]{1,0:T(8,128)} %param.9) | copy-start | bytes 786436
  6.7 13.4 %collective-permute-start = (f32[3,16,64,5]{2,1,3,0:T(8,128)S(1)}, f32[3,16,64,5]{2,1,3,0:T(8,128)}, u32[]{:S(2)}, u32[]{:S(2)}) collective-permute-start(f32[3,16,64,5]{2,1,3,0:T(8,128)S(1)} %copy.29), channel_id=1, source_target_pairs={{0,1},{2,3},{4,5},{6,7},{8,9},{10,11},{12,13},{14,15},{16,17},{18,... | collective-permute-start | bytes 184328 | tf_op jit(solution)/shard_map/ppermute | solution.py:73
  14.2 8.5 %collective-permute-start.1 = (f32[3,16,64,5]{2,1,3,0:T(8,128)}, f32[3,16,64,5]{2,1,3,0:T(8,128)}, u32[]{:S(2)}, u32[]{:S(2)}) collective-permute-start(f32[3,16,64,5]{2,1,3,0:T(8,128)} %copy.30), channel_id=1, source_target_pairs={{1,0},{3,2},{5,4},{7,6},{9,8},{11,10},{13,12},{15,14},{17,16},{19,... | collective-permute-start | bytes 184328 | tf_op jit(solution)/shard_map/ppermute | solution.py:75
  27.8 8.8 %collective-permute-start.2 = (f32[3,16,5,266]{3,1,2,0:T(8,128)}, f32[3,16,5,266]{3,1,2,0:T(8,128)}, u32[]{:S(2)}, u32[]{:S(2)}) collective-permute-start(f32[3,16,5,266]{3,1,2,0:T(8,128)} %copy.33), channel_id=1, source_target_pairs={{0,2},{2,4},{4,6},{6,8},{8,10},{10,12},{12,14},{14,16},{16,18},{18... | collective-permute-start | bytes 766088 | tf_op jit(solution)/shard_map/ppermute | solution.py:73
  31.8 9.1 %collective-permute-start.3 = (f32[3,16,5,266]{3,1,2,0:T(8,128)}, f32[3,16,5,266]{3,1,2,0:T(8,128)}, u32[]{:S(2)}, u32[]{:S(2)}) collective-permute-start(f32[3,16,5,266]{3,1,2,0:T(8,128)} %copy.34), channel_id=1, source_target_pairs={{2,0},{4,2},{6,4},{8,6},{10,8},{12,10},{14,12},{16,14},{18,16},{20... | collective-permute-start | bytes 766088 | tf_op jit(solution)/shard_map/ppermute | solution.py:75
  46.7 40.6 %collective-permute-start.4 = (f32[3,5,74,266]{3,2,1,0:T(8,128)}, f32[3,5,74,266]{3,2,1,0:T(8,128)}, u32[]{:S(2)}, u32[]{:S(2)}) collective-permute-start(f32[3,5,74,266]{3,2,1,0:T(8,128)} %get-tuple-element.21), channel_id=1, source_target_pairs={{0,32},{32,64},{64,96},{1,33},{33,65},{65,97},{2,34},{34,66},{66,9... | collective-permute-start | bytes 3543128 | tf_op jit(solution)/shard_map/ppermute | solution.py:73
  51.5 41.2 %collective-permute-start.5 = (f32[3,5,74,266]{3,2,1,0:T(8,128)}, f32[3,5,74,266]{3,2,1,0:T(8,128)}, u32[]{:S(2)}, u32[]{:S(2)}) collective-permute-start(f32[3,5,74,266]{3,2,1,0:T(8,128)} %get-tuple-element.22), channel_id=1, source_target_pairs={{32,0},{64,32},{96,64},{33,1},{65,33},{97,65},{34,2},{66,34},{98,6... | collective-permute-start | bytes 3543128 | tf_op jit(solution)/shard_map/ppermute | solution.py:75
  53.6 39.1 %copy-start.4 = (f32[3,16,64,5]{3,2,1,0:T(8,128)S(1)}, f32[3,16,64,5]{3,2,1,0:T(8,128)}, u32[]{:S(2)}) copy-start(f32[3,16,64,5]{3,2,1,0:T(8,128)} %copy.31) | copy-start | bytes 184324
  137.6 33.7 %copy-start.10 = (f32[64,128]{1,0:T(8,128)S(1)}, f32[64,128]{1,0:T(8,128)}, u32[]{:S(2)}) copy-start(f32[64,128]{1,0:T(8,128)} %fusion.89) | copy-start | bytes 98308
  137.6 33.7 %copy-start.14 = (s32[128]{0:T(128)S(1)}, s32[128]{0:T(128)}, u32[]{:S(2)}) copy-start(s32[128]{0:T(128)} %get-tuple-element.49) | copy-start | bytes 1540
  137.6 33.7 %copy-start.15 = (s32[128]{0:T(128)S(1)}, s32[128]{0:T(128)}, u32[]{:S(2)}) copy-start(s32[128]{0:T(128)} %get-tuple-element.50) | copy-start | bytes 1540
  137.6 33.7 %copy-start.16 = (pred[128]{0:T(512)(128)(4,1)S(1)}, pred[128]{0:T(512)(128)(4,1)}, u32[]{:S(2)}) copy-start(pred[128]{0:T(512)(128)(4,1)} %compare_and_fusion) | copy-start | bytes 388
  137.8 9.9 %collective-permute-start.6 = (f32[2,8,32,4]{3,2,1,0:T(8,128)S(1)}, f32[2,8,32,4]{3,2,1,0:T(8,128)S(1)}, u32[]{:S(2)}, u32[]{:S(2)}) collective-permute-start(f32[2,8,32,4]{3,2,1,0:T(8,128)S(1)} %get-tuple-element.35), channel_id=1, source_target_pairs={{0,1},{2,3},{4,5},{6,7},{8,9},{10,11},{12,13},{14,15},{16,17},{18,... | collective-permute-start | bytes 24584 | tf_op jit(solution)/shard_map/ppermute | solution.py:73
  144.1 9.2 %collective-permute-start.7 = (f32[2,8,32,4]{3,2,1,0:T(8,128)S(1)}, f32[2,8,32,4]{3,2,1,0:T(8,128)S(1)}, u32[]{:S(2)}, u32[]{:S(2)}) collective-permute-start(f32[2,8,32,4]{3,2,1,0:T(8,128)S(1)} %get-tuple-element.36), channel_id=1, source_target_pairs={{1,0},{3,2},{5,4},{7,6},{9,8},{11,10},{13,12},{15,14},{17,16},{19,... | collective-permute-start | bytes 24584 | tf_op jit(solution)/shard_map/ppermute | solution.py:75
  153.4 10.0 %collective-permute-start.8 = (f32[2,8,4,136]{3,2,1,0:T(4,128)S(1)}, f32[2,8,4,136]{3,2,1,0:T(4,128)S(1)}, u32[]{:S(2)}, u32[]{:S(2)}) collective-permute-start(f32[2,8,4,136]{3,2,1,0:T(4,128)S(1)} %get-tuple-element.29), channel_id=1, source_target_pairs={{0,2},{2,4},{4,6},{6,8},{8,10},{10,12},{12,14},{14,16},{16,18},{18... | collective-permute-start | bytes 104456 | tf_op jit(solution)/shard_map/ppermute | solution.py:73
  161.5 5.6 %collective-permute-start.9 = (f32[2,8,4,136]{3,2,1,0:T(4,128)S(1)}, f32[2,8,4,136]{3,2,1,0:T(4,128)S(1)}, u32[]{:S(2)}, u32[]{:S(2)}) collective-permute-start(f32[2,8,4,136]{3,2,1,0:T(4,128)S(1)} %get-tuple-element.30), channel_id=1, source_target_pairs={{2,0},{4,2},{6,4},{8,6},{10,8},{12,10},{14,12},{16,14},{18,16},{20... | collective-permute-start | bytes 104456 | tf_op jit(solution)/shard_map/ppermute | solution.py:75
  167.5 7.8 %collective-permute-start.10 = (f32[2,4,40,136]{3,2,1,0:T(8,128)S(1)}, f32[2,4,40,136]{3,2,1,0:T(8,128)S(1)}, u32[]{:S(2)}, u32[]{:S(2)}) collective-permute-start(f32[2,4,40,136]{3,2,1,0:T(8,128)S(1)} %get-tuple-element.31), channel_id=1, source_target_pairs={{0,32},{32,64},{64,96},{1,33},{33,65},{65,97},{2,34},{34,66},{66,9... | collective-permute-start | bytes 522248 | tf_op jit(solution)/shard_map/ppermute | solution.py:73
  169.8 9.6 %collective-permute-start.11 = (f32[2,4,40,136]{3,2,1,0:T(8,128)S(1)}, f32[2,4,40,136]{3,2,1,0:T(8,128)S(1)}, u32[]{:S(2)}, u32[]{:S(2)}) collective-permute-start(f32[2,4,40,136]{3,2,1,0:T(8,128)S(1)} %get-tuple-element.32), channel_id=1, source_target_pairs={{32,0},{64,32},{96,64},{33,1},{65,33},{97,65},{34,2},{66,34},{98,6... | collective-permute-start | bytes 522248 | tf_op jit(solution)/shard_map/ppermute | solution.py:75
  185.9 3.2 %collective-permute-start.12 = (f32[2,4,16,4]{3,2,1,0:T(8,128)S(1)}, f32[2,4,16,4]{3,2,1,0:T(8,128)S(1)}, u32[]{:S(2)}, u32[]{:S(2)}) collective-permute-start(f32[2,4,16,4]{3,2,1,0:T(8,128)S(1)} %get-tuple-element.39), channel_id=1, source_target_pairs={{0,1},{2,3},{4,5},{6,7},{8,9},{10,11},{12,13},{14,15},{16,17},{18,... | collective-permute-start | bytes 6152 | tf_op jit(solution)/shard_map/ppermute | solution.py:73
  187.7 7.0 %collective-permute-start.13 = (f32[2,4,16,4]{3,2,1,0:T(8,128)S(1)}, f32[2,4,16,4]{3,2,1,0:T(8,128)S(1)}, u32[]{:S(2)}, u32[]{:S(2)}) collective-permute-start(f32[2,4,16,4]{3,2,1,0:T(8,128)S(1)} %get-tuple-element.40), channel_id=1, source_target_pairs={{1,0},{3,2},{5,4},{7,6},{9,8},{11,10},{13,12},{15,14},{17,16},{19,... | collective-permute-start | bytes 6152 | tf_op jit(solution)/shard_map/ppermute | solution.py:75
  194.8 5.5 %collective-permute-start.14 = (f32[2,4,4,72]{3,2,1,0:T(4,128)S(1)}, f32[2,4,4,72]{3,2,1,0:T(4,128)S(1)}, u32[]{:S(2)}, u32[]{:S(2)}) collective-permute-start(f32[2,4,4,72]{3,2,1,0:T(4,128)S(1)} %get-tuple-element.37), channel_id=1, source_target_pairs={{0,2},{2,4},{4,6},{6,8},{8,10},{10,12},{12,14},{14,16},{16,18},{18... | collective-permute-start | bytes 27656 | tf_op jit(solution)/shard_map/ppermute | solution.py:73
  198.3 5.1 %collective-permute-start.15 = (f32[2,4,4,72]{3,2,1,0:T(4,128)S(1)}, f32[2,4,4,72]{3,2,1,0:T(4,128)S(1)}, u32[]{:S(2)}, u32[]{:S(2)}) collective-permute-start(f32[2,4,4,72]{3,2,1,0:T(4,128)S(1)} %get-tuple-element.38), channel_id=1, source_target_pairs={{2,0},{4,2},{6,4},{8,6},{10,8},{12,10},{14,12},{16,14},{18,16},{20... | collective-permute-start | bytes 27656 | tf_op jit(solution)/shard_map/ppermute | solution.py:75
  203.5 4.9 %collective-permute-start.16 = (f32[2,4,24,72]{3,2,1,0:T(8,128)S(1)}, f32[2,4,24,72]{3,2,1,0:T(8,128)S(1)}, u32[]{:S(2)}, u32[]{:S(2)}) collective-permute-start(f32[2,4,24,72]{3,2,1,0:T(8,128)S(1)} %pad_maximum_fusion.18), channel_id=1, source_target_pairs={{0,32},{32,64},{64,96},{1,33},{33,65},{65,97},{2,34},{34,66},{66,9... | collective-permute-start | bytes 165896 | tf_op jit(solution)/shard_map/ppermute | solution.py:73
  206.7 5.4 %collective-permute-start.17 = (f32[2,4,24,72]{3,2,1,0:T(8,128)S(1)}, f32[2,4,24,72]{3,2,1,0:T(8,128)S(1)}, u32[]{:S(2)}, u32[]{:S(2)}) collective-permute-start(f32[2,4,24,72]{3,2,1,0:T(8,128)S(1)} %pad_maximum_fusion.18), channel_id=1, source_target_pairs={{32,0},{64,32},{96,64},{33,1},{65,33},{97,65},{34,2},{66,34},{98,6... | collective-permute-start | bytes 165896 | tf_op jit(solution)/shard_map/ppermute | solution.py:75
  (15 other events, 107.4 us)

commit v3 on v2

--- a/solution.py
+++ b/solution.py
@@ -135,7 +135,9 @@
     partial_sums = jnp.dot(
         coarse_defect.reshape(1, cells), one_hot, precision=lax.Precision.HIGHEST
     ).reshape(NAGG)
-    summed = lax.psum(partial_sums, ("gx", "gy", "gz"))
+    summed = lax.psum(partial_sums, "gz")
+    summed = lax.psum(summed, "gx")
+    summed = lax.psum(summed, "gy")
     group_cells = (
         coarse_source.size * lax.axis_size("gx") * lax.axis_size("gy") * lax.axis_size("gz") // NAGG
     )

time: 293 us -> 267 us (0.911)
  blocking collectives: 67.2 us -> 41.1 us
    psum x1 -> x3, blocking collectives: 67.2 us -> 41.1 us  [the longest x1 29.5 us: shards(): summed = lax.psum(summed, 'gy')]
  transfers between devices with their start and end apart: 18 -> 18, of which waited for: 12 -> 12; matrix products, arithmetic and copies ran while one was open for 7% -> 8% of each run, Pallas kernels for 0% -> 0%
where the time goes in v3:
time: 267 us; the launch traced here: 262 us
  other arithmetic  68.7 us (26%)
  waiting for transfers between devices  67.9 us (25%)
  starting transfers between devices  53.4 us (20%)
  blocking collectives  41.1 us (15%)
  local copies, waits for them, and re-layouts  15.1 us (6%)
  matrix products  13.6 us (5%)
    ppermute x9, starting transfers between devices, exchange(): lax.ppermute(tail, axis, [(i, i + 1) for i in range(count - 1)])  39.5 us
    ppermute x9, waiting for transfers between devices, exchange(): lax.ppermute(head, axis, [(i + 1, i) for i in range(count - 1)])  34.5 us
    ppermute x9, waiting for transfers between devices, exchange(): lax.ppermute(tail, axis, [(i, i + 1) for i in range(count - 1)])  33.5 us
    select_n x10, other arithmetic, smooth_wide(): current = jnp.where(crop(mask, step), current, 0.0)  29.9 us
    psum x1, blocking collectives, shards(): summed = lax.psum(summed, 'gy')  29.5 us
    ppermute x9, starting transfers between devices, exchange(): lax.ppermute(head, axis, [(i + 1, i) for i in range(count - 1)])  13.9 us
    concatenate x5, other arithmetic, exchange(): jnp.concatenate([lax.ppermute(tail, axis, [(i, i + 1) for i in range(coun...  12.1 us
    slice x4, other arithmetic, exchange(): lax.slice_in_dim(stack, stack.shape[dim] - width, stack.shape[dim], axis=...  6.49 us
  transfers between devices with their start and end apart: 18, of which 12 were waited for; matrix products, arithmetic and copies ran while one was open for 8% of the time, Pallas kernels for 0%

profile of v3, /device:TPU:1, one launch (start us, length us, event | category | flops | bytes accessed | tf_op | source)
XLA Modules:
  0.0 261.7 jit_solution(15686289829892610653)
XLA Ops:
  6.7 6.3 %collective-permute-start = (f32[3,16,64,5]{2,1,3,0:T(8,128)S(1)}, f32[3,16,64,5]{2,1,3,0:T(8,128)}, u32[]{:S(2)}, u32[]{:S(2)}) collective-permute-start(f32[3,16,64,5]{2,1,3,0:T(8,128)S(1)} %copy.29), channel_id=1, source_target_pairs={{0,1},{2,3},{4,5},{6,7},{8,9},{10,11},{12,13},{14,15},{16,17},{18,... | collective-permute-start | bytes 184328 | tf_op jit(solution)/shard_map/ppermute | solution.py:73
  42.1 4.5 %pad_maximum_fusion.8 = (f32[3,5,74,266]{3,2,1,0:T(8,128)}, f32[3,5,74,266]{3,2,1,0:T(8,128)}) fusion(f32[3,16,5,266]{3,2,1,0:T(8,128)S(1)} %copy.36, f32[3,16,5,266]{3,2,1,0:T(8,128)S(1)} %copy.35, f32[3,16,64,5]{3,2,1,0:T(8,128)} %copy.32, f32[3,16,64,5]{3,2,1,0:T(8,128)S(1)} %copy-done.3, f32[1,16,64,256]{3,2,1,0:T(8,128)S(1)} %bitcast.59, ...), kind=kLoop, calls=%fused_computation.59 | loop fusion | flops 3543120 | bytes 6141408 | tf_op jit(solution)/shard_map/slice | solution.py:70
  46.6 4.9 %collective-permute-start.4 = (f32[3,5,74,266]{3,2,1,0:T(8,128)}, f32[3,5,74,266]{3,2,1,0:T(8,128)}, u32[]{:S(2)}, u32[]{:S(2)}) collective-permute-start(f32[3,5,74,266]{3,2,1,0:T(8,128)} %get-tuple-element.21), channel_id=1, source_target_pairs={{0,32},{32,64},{64,96},{1,33},{33,65},{65,97},{2,34},{34,66},{66,9... | collective-permute-start | bytes 3543128 | tf_op jit(solution)/shard_map/ppermute | solution.py:73
  59.8 27.4 %collective-permute-done.4 = f32[3,5,74,266]{3,2,1,0:T(8,128)} collective-permute-done((f32[3,5,74,266]{3,2,1,0:T(8,128)}, f32[3,5,74,266]{3,2,1,0:T(8,128)}, u32[]{:S(2)}, u32[]{:S(2)}) %collective-permute-start.4) | collective-permute-done | bytes 1181072 | tf_op jit(solution)/shard_map/ppermute | solution.py:73
  87.2 5.4 %collective-permute-done.5 = f32[3,5,74,266]{3,2,1,0:T(8,128)} collective-permute-done((f32[3,5,74,266]{3,2,1,0:T(8,128)}, f32[3,5,74,266]{3,2,1,0:T(8,128)}, u32[]{:S(2)}, u32[]{:S(2)}) %collective-permute-start.5) | collective-permute-done | bytes 1181072 | tf_op jit(solution)/shard_map/ppermute | solution.py:75
  92.6 11.2 %pad_maximum_fusion = f32[3,26,74,266]{3,2,1,0:T(8,128)} fusion(f32[3,5,74,266]{3,2,1,0:T(8,128)} %collective-permute-done.5, f32[3,16,5,266]{3,2,1,0:T(8,128)} %copy-done.7, f32[3,16,64,5]{3,2,1,0:T(8,128)} %copy.32, f32[1,16,64,256]{3,2,1,0:T(8,128)S(1)} %bitcast.60, f32[1,16,64,256]{3,2,1,0:T(8,128)S(1)} %bitcast.64, f32[1,16,64,256]{3,2,1,0:T(8,128)S(1)} %bitcast.68, ...), kind=kLoop, calls=%fused_computation.2 | loop fusion | flops 12282816 | bytes 12282816 | tf_op jit(solution)/shard_map/concatenate | solution.py:71
  103.9 4.5 %fusion.2 = (f32[26,74,266]{2,1,0:T(8,128)S(1)}, f32[26,74,266]{2,1,0:T(8,128)S(1)}, f32[26,74,266]{2,1,0:T(8,128)S(1)}) fusion(f32[3,26,74,266]{3,2,1,0:T(8,128)} %pad_maximum_fusion), kind=kLoop, calls=%fused_computation.5 | loop fusion | flops 511784 | bytes 12282816 | tf_op jit(solution)/shard_map/add | solution.py:120
  108.4 7.2 %fusion.8 = f32[24,72,264]{2,1,0:T(8,128)S(1)} fusion(f32[26,74,266]{2,1,0:T(8,128)S(1)} %get-tuple-element.20, f32[26,74,266]{2,1,0:T(8,128)S(1)} %get-tuple-element.19, f32[26,74,266]{2,1,0:T(8,128)S(1)} %get-tuple-element.18, pred[26,74,266]{2,1,0:T(8,128)(4,1)S(1)} %broadcast_and_fusion), kind=kLoop, calls=%fused_computation.15 | loop fusion | flops 5474304 | bytes 18703872 | tf_op jit(solution)/shard_map/jit(_where)/select_n | solution.py:101
  115.6 6.5 %fusion.14 = f32[22,70,262]{2,1,0:T(8,128)S(1)} fusion(f32[24,72,264]{2,1,0:T(8,128)S(1)} %fusion.8, f32[26,74,266]{2,1,0:T(8,128)S(1)} %get-tuple-element.19, f32[26,74,266]{2,1,0:T(8,128)S(1)} %get-tuple-element.18, pred[26,74,266]{2,1,0:T(8,128)(4,1)S(1)} %broadcast_and_fusion), kind=kLoop, calls=%fused_computation.26 | loop fusion | flops 4841760 | bytes 16542680 | tf_op jit(solution)/shard_map/jit(_where)/select_n | solution.py:101
  122.1 6.2 %fusion.20 = f32[20,68,260]{2,1,0:T(8,128)S(1)} fusion(f32[22,70,262]{2,1,0:T(8,128)S(1)} %fusion.14, f32[26,74,266]{2,1,0:T(8,128)S(1)} %get-tuple-element.19, f32[26,74,266]{2,1,0:T(8,128)S(1)} %get-tuple-element.18, pred[26,74,266]{2,1,0:T(8,128)(4,1)S(1)} %broadcast_and_fusion), kind=kLoop, calls=%fused_computation.37 | loop fusion | flops 4243200 | bytes 14497600 | tf_op jit(solution)/shard_map/jit(_where)/select_n | solution.py:101
  128.3 5.4 %fusion.26 = f32[18,66,258]{2,1,0:T(8,128)S(1)} fusion(f32[20,68,260]{2,1,0:T(8,128)S(1)} %fusion.20, f32[26,74,266]{2,1,0:T(8,128)S(1)} %get-tuple-element.19, f32[26,74,266]{2,1,0:T(8,128)S(1)} %get-tuple-element.18, pred[26,74,266]{2,1,0:T(8,128)(4,1)S(1)} %broadcast_and_fusion), kind=kLoop, calls=%fused_computation.48 | loop fusion | flops 3678048 | bytes 12566664 | tf_op jit(solution)/shard_map/jit(_where)/select_n | solution.py:101
  137.7 6.2 %collective-permute-start.6 = (f32[2,8,32,4]{3,2,1,0:T(8,128)S(1)}, f32[2,8,32,4]{3,2,1,0:T(8,128)S(1)}, u32[]{:S(2)}, u32[]{:S(2)}) collective-permute-start(f32[2,8,32,4]{3,2,1,0:T(8,128)S(1)} %get-tuple-element.35), channel_id=1, source_target_pairs={{0,1},{2,3},{4,5},{6,7},{8,9},{10,11},{12,13},{14,15},{16,17},{18,... | collective-permute-start | bytes 24584 | tf_op jit(solution)/shard_map/ppermute | solution.py:73
  147.6 5.6 %collective-permute-done.7 = f32[2,8,32,4]{3,2,1,0:T(8,128)S(1)} collective-permute-done((f32[2,8,32,4]{3,2,1,0:T(8,128)S(1)}, f32[2,8,32,4]{3,2,1,0:T(8,128)S(1)}, u32[]{:S(2)}, u32[]{:S(2)}) %collective-permute-start.7) | collective-permute-done | bytes 8224 | tf_op jit(solution)/shard_map/ppermute | solution.py:75
  153.3 8.1 %collective-permute-start.8 = (f32[2,8,4,136]{3,2,1,0:T(4,128)S(1)}, f32[2,8,4,136]{3,2,1,0:T(4,128)S(1)}, u32[]{:S(2)}, u32[]{:S(2)}) collective-permute-start(f32[2,8,4,136]{3,2,1,0:T(4,128)S(1)} %get-tuple-element.29), channel_id=1, source_target_pairs={{0,2},{2,4},{4,6},{6,8},{8,10},{10,12},{12,14},{14,16},{16,18},{18... | collective-permute-start | bytes 104456 | tf_op jit(solution)/shard_map/ppermute | solution.py:73
  163.4 3.6 %collective-permute-done.9 = f32[2,8,4,136]{3,2,1,0:T(4,128)S(1)} collective-permute-done((f32[2,8,4,136]{3,2,1,0:T(4,128)S(1)}, f32[2,8,4,136]{3,2,1,0:T(4,128)S(1)}, u32[]{:S(2)}, u32[]{:S(2)}) %collective-permute-start.9) | collective-permute-done | bytes 34848 | tf_op jit(solution)/shard_map/ppermute | solution.py:75
  171.6 3.6 %collective-permute-done.10 = f32[2,4,40,136]{3,2,1,0:T(8,128)S(1)} collective-permute-done((f32[2,4,40,136]{3,2,1,0:T(8,128)S(1)}, f32[2,4,40,136]{3,2,1,0:T(8,128)S(1)}, u32[]{:S(2)}, u32[]{:S(2)}) %collective-permute-start.10) | collective-permute-done | bytes 174112 | tf_op jit(solution)/shard_map/ppermute | solution.py:73
  175.2 4.1 %collective-permute-done.11 = f32[2,4,40,136]{3,2,1,0:T(8,128)S(1)} collective-permute-done((f32[2,4,40,136]{3,2,1,0:T(8,128)S(1)}, f32[2,4,40,136]{3,2,1,0:T(8,128)S(1)}, u32[]{:S(2)}, u32[]{:S(2)}) %collective-permute-start.11) | collective-permute-done | bytes 174112 | tf_op jit(solution)/shard_map/ppermute | solution.py:75
  189.0 5.6 %collective-permute-done.13 = f32[2,4,16,4]{3,2,1,0:T(8,128)S(1)} collective-permute-done((f32[2,4,16,4]{3,2,1,0:T(8,128)S(1)}, f32[2,4,16,4]{3,2,1,0:T(8,128)S(1)}, u32[]{:S(2)}, u32[]{:S(2)}) %collective-permute-start.13) | collective-permute-done | bytes 2080 | tf_op jit(solution)/shard_map/ppermute | solution.py:75
  194.7 3.5 %collective-permute-start.14 = (f32[2,4,4,72]{3,2,1,0:T(4,128)S(1)}, f32[2,4,4,72]{3,2,1,0:T(4,128)S(1)}, u32[]{:S(2)}, u32[]{:S(2)}) collective-permute-start(f32[2,4,4,72]{3,2,1,0:T(4,128)S(1)} %get-tuple-element.37), channel_id=1, source_target_pairs={{0,2},{2,4},{4,6},{6,8},{8,10},{10,12},{12,14},{14,16},{16,18},{18... | collective-permute-start | bytes 27656 | tf_op jit(solution)/shard_map/ppermute | solution.py:73
  208.3 3.7 %collective-permute-done.17 = f32[2,4,24,72]{3,2,1,0:T(8,128)S(1)} collective-permute-done((f32[2,4,24,72]{3,2,1,0:T(8,128)S(1)}, f32[2,4,24,72]{3,2,1,0:T(8,128)S(1)}, u32[]{:S(2)}, u32[]{:S(2)}) %collective-permute-start.17) | collective-permute-done | bytes 55328 | tf_op jit(solution)/shard_map/ppermute | solution.py:75
  214.0 5.3 %fusion = f32[1,1024]{1,0:T(1,128)S(1)} fusion(f32[4096,1]{0,1:T(1,128)S(1)} %reshape.280, s32[4096]{0:T(1024)S(1)} %eq.38), kind=kOutput, calls=%fused_computation.1 | convolution fusion | flops 54525952 | bytes 36864 | tf_op jit(solution)/shard_map/dot_general | solution.py:135
  219.3 5.5 %psum.21 = f32[1024]{0:T(1024)S(1)} all-reduce(f32[1024]{0:T(1024)S(1)} %bitcast.97), channel_id=1, replica_groups=mesh['gx'=4,'gy'=16,'gz'=2] {'gz'}, use_global_device_ids=true, to_apply=%region_0.1 | all-reduce | flops 1024 | bytes 8192 | tf_op jit(solution)/shard_map/psum | solution.py:138
  224.8 6.1 %psum.22 = f32[1024]{0:T(1024)S(1)} all-reduce(f32[1024]{0:T(1024)S(1)} %psum.21), channel_id=1, replica_groups=mesh['gx'=4,'gy'=16,'gz'=2] {'gx'}, use_global_device_ids=true, to_apply=%region_1.2 | all-reduce | flops 1024 | bytes 8192 | tf_op jit(solution)/shard_map/psum | solution.py:139
  230.9 29.5 %psum.23 = f32[1024]{0:T(1024)S(1)} all-reduce(f32[1024]{0:T(1024)S(1)} %psum.22), channel_id=1, replica_groups=mesh['gx'=4,'gy'=16,'gz'=2] {'gy'}, use_global_device_ids=true, to_apply=%region_2.3 | all-reduce | flops 1024 | bytes 8192 | tf_op jit(solution)/shard_map/psum | solution.py:140
  (135 shorter events, 79.7 us)
Async XLA Ops:
  0.6 259.8 %copy-start = (f32[64,1024]{1,0:T(8,128)S(1)}, f32[64,1024]{1,0:T(8,128)}, u32[]{:S(2)}) copy-start(f32[64,1024]{1,0:T(8,128)} %param.9) | copy-start | bytes 786436
  6.7 13.3 %collective-permute-start = (f32[3,16,64,5]{2,1,3,0:T(8,128)S(1)}, f32[3,16,64,5]{2,1,3,0:T(8,128)}, u32[]{:S(2)}, u32[]{:S(2)}) collective-permute-start(f32[3,16,64,5]{2,1,3,0:T(8,128)S(1)} %copy.29), channel_id=1, source_target_pairs={{0,1},{2,3},{4,5},{6,7},{8,9},{10,11},{12,13},{14,15},{16,17},{18,... | collective-permute-start | bytes 184328 | tf_op jit(solution)/shard_map/ppermute | solution.py:73
  14.2 8.5 %collective-permute-start.1 = (f32[3,16,64,5]{2,1,3,0:T(8,128)}, f32[3,16,64,5]{2,1,3,0:T(8,128)}, u32[]{:S(2)}, u32[]{:S(2)}) collective-permute-start(f32[3,16,64,5]{2,1,3,0:T(8,128)} %copy.30), channel_id=1, source_target_pairs={{1,0},{3,2},{5,4},{7,6},{9,8},{11,10},{13,12},{15,14},{17,16},{19,... | collective-permute-start | bytes 184328 | tf_op jit(solution)/shard_map/ppermute | solution.py:75
  27.8 8.8 %collective-permute-start.2 = (f32[3,16,5,266]{3,1,2,0:T(8,128)}, f32[3,16,5,266]{3,1,2,0:T(8,128)}, u32[]{:S(2)}, u32[]{:S(2)}) collective-permute-start(f32[3,16,5,266]{3,1,2,0:T(8,128)} %copy.33), channel_id=1, source_target_pairs={{0,2},{2,4},{4,6},{6,8},{8,10},{10,12},{12,14},{14,16},{16,18},{18... | collective-permute-start | bytes 766088 | tf_op jit(solution)/shard_map/ppermute | solution.py:73
  31.8 9.1 %collective-permute-start.3 = (f32[3,16,5,266]{3,1,2,0:T(8,128)}, f32[3,16,5,266]{3,1,2,0:T(8,128)}, u32[]{:S(2)}, u32[]{:S(2)}) collective-permute-start(f32[3,16,5,266]{3,1,2,0:T(8,128)} %copy.34), channel_id=1, source_target_pairs={{2,0},{4,2},{6,4},{8,6},{10,8},{12,10},{14,12},{16,14},{18,16},{20... | collective-permute-start | bytes 766088 | tf_op jit(solution)/shard_map/ppermute | solution.py:75
  46.6 40.6 %collective-permute-start.4 = (f32[3,5,74,266]{3,2,1,0:T(8,128)}, f32[3,5,74,266]{3,2,1,0:T(8,128)}, u32[]{:S(2)}, u32[]{:S(2)}) collective-permute-start(f32[3,5,74,266]{3,2,1,0:T(8,128)} %get-tuple-element.21), channel_id=1, source_target_pairs={{0,32},{32,64},{64,96},{1,33},{33,65},{65,97},{2,34},{34,66},{66,9... | collective-permute-start | bytes 3543128 | tf_op jit(solution)/shard_map/ppermute | solution.py:73
  51.5 41.2 %collective-permute-start.5 = (f32[3,5,74,266]{3,2,1,0:T(8,128)}, f32[3,5,74,266]{3,2,1,0:T(8,128)}, u32[]{:S(2)}, u32[]{:S(2)}) collective-permute-start(f32[3,5,74,266]{3,2,1,0:T(8,128)} %get-tuple-element.22), channel_id=1, source_target_pairs={{32,0},{64,32},{96,64},{33,1},{65,33},{97,65},{34,2},{66,34},{98,6... | collective-permute-start | bytes 3543128 | tf_op jit(solution)/shard_map/ppermute | solution.py:75
  53.5 39.1 %copy-start.4 = (f32[3,16,64,5]{3,2,1,0:T(8,128)S(1)}, f32[3,16,64,5]{3,2,1,0:T(8,128)}, u32[]{:S(2)}) copy-start(f32[3,16,64,5]{3,2,1,0:T(8,128)} %copy.31) | copy-start | bytes 184324
  137.5 33.7 %copy-start.10 = (f32[64,128]{1,0:T(8,128)S(1)}, f32[64,128]{1,0:T(8,128)}, u32[]{:S(2)}) copy-start(f32[64,128]{1,0:T(8,128)} %fusion.89) | copy-start | bytes 98308
  137.5 33.7 %copy-start.14 = (s32[128]{0:T(128)S(1)}, s32[128]{0:T(128)}, u32[]{:S(2)}) copy-start(s32[128]{0:T(128)} %get-tuple-element.49) | copy-start | bytes 1540
  137.5 33.7 %copy-start.15 = (s32[128]{0:T(128)S(1)}, s32[128]{0:T(128)}, u32[]{:S(2)}) copy-start(s32[128]{0:T(128)} %get-tuple-element.50) | copy-start | bytes 1540
  137.6 33.7 %copy-start.16 = (pred[128]{0:T(512)(128)(4,1)S(1)}, pred[128]{0:T(512)(128)(4,1)}, u32[]{:S(2)}) copy-start(pred[128]{0:T(512)(128)(4,1)} %compare_and_fusion) | copy-start | bytes 388
  137.7 9.8 %collective-permute-start.6 = (f32[2,8,32,4]{3,2,1,0:T(8,128)S(1)}, f32[2,8,32,4]{3,2,1,0:T(8,128)S(1)}, u32[]{:S(2)}, u32[]{:S(2)}) collective-permute-start(f32[2,8,32,4]{3,2,1,0:T(8,128)S(1)} %get-tuple-element.35), channel_id=1, source_target_pairs={{0,1},{2,3},{4,5},{6,7},{8,9},{10,11},{12,13},{14,15},{16,17},{18,... | collective-permute-start | bytes 24584 | tf_op jit(solution)/shard_map/ppermute | solution.py:73
  144.0 9.2 %collective-permute-start.7 = (f32[2,8,32,4]{3,2,1,0:T(8,128)S(1)}, f32[2,8,32,4]{3,2,1,0:T(8,128)S(1)}, u32[]{:S(2)}, u32[]{:S(2)}) collective-permute-start(f32[2,8,32,4]{3,2,1,0:T(8,128)S(1)} %get-tuple-element.36), channel_id=1, source_target_pairs={{1,0},{3,2},{5,4},{7,6},{9,8},{11,10},{13,12},{15,14},{17,16},{19,... | collective-permute-start | bytes 24584 | tf_op jit(solution)/shard_map/ppermute | solution.py:75
  153.3 10.1 %collective-permute-start.8 = (f32[2,8,4,136]{3,2,1,0:T(4,128)S(1)}, f32[2,8,4,136]{3,2,1,0:T(4,128)S(1)}, u32[]{:S(2)}, u32[]{:S(2)}) collective-permute-start(f32[2,8,4,136]{3,2,1,0:T(4,128)S(1)} %get-tuple-element.29), channel_id=1, source_target_pairs={{0,2},{2,4},{4,6},{6,8},{8,10},{10,12},{12,14},{14,16},{16,18},{18... | collective-permute-start | bytes 104456 | tf_op jit(solution)/shard_map/ppermute | solution.py:73
  161.5 5.6 %collective-permute-start.9 = (f32[2,8,4,136]{3,2,1,0:T(4,128)S(1)}, f32[2,8,4,136]{3,2,1,0:T(4,128)S(1)}, u32[]{:S(2)}, u32[]{:S(2)}) collective-permute-start(f32[2,8,4,136]{3,2,1,0:T(4,128)S(1)} %get-tuple-element.30), channel_id=1, source_target_pairs={{2,0},{4,2},{6,4},{8,6},{10,8},{12,10},{14,12},{16,14},{18,16},{20... | collective-permute-start | bytes 104456 | tf_op jit(solution)/shard_map/ppermute | solution.py:75
  167.4 7.8 %collective-permute-start.10 = (f32[2,4,40,136]{3,2,1,0:T(8,128)S(1)}, f32[2,4,40,136]{3,2,1,0:T(8,128)S(1)}, u32[]{:S(2)}, u32[]{:S(2)}) collective-permute-start(f32[2,4,40,136]{3,2,1,0:T(8,128)S(1)} %get-tuple-element.31), channel_id=1, source_target_pairs={{0,32},{32,64},{64,96},{1,33},{33,65},{65,97},{2,34},{34,66},{66,9... | collective-permute-start | bytes 522248 | tf_op jit(solution)/shard_map/ppermute | solution.py:73
  169.7 9.6 %collective-permute-start.11 = (f32[2,4,40,136]{3,2,1,0:T(8,128)S(1)}, f32[2,4,40,136]{3,2,1,0:T(8,128)S(1)}, u32[]{:S(2)}, u32[]{:S(2)}) collective-permute-start(f32[2,4,40,136]{3,2,1,0:T(8,128)S(1)} %get-tuple-element.32), channel_id=1, source_target_pairs={{32,0},{64,32},{96,64},{33,1},{65,33},{97,65},{34,2},{66,34},{98,6... | collective-permute-start | bytes 522248 | tf_op jit(solution)/shard_map/ppermute | solution.py:75
  185.8 3.2 %collective-permute-start.12 = (f32[2,4,16,4]{3,2,1,0:T(8,128)S(1)}, f32[2,4,16,4]{3,2,1,0:T(8,128)S(1)}, u32[]{:S(2)}, u32[]{:S(2)}) collective-permute-start(f32[2,4,16,4]{3,2,1,0:T(8,128)S(1)} %get-tuple-element.39), channel_id=1, source_target_pairs={{0,1},{2,3},{4,5},{6,7},{8,9},{10,11},{12,13},{14,15},{16,17},{18,... | collective-permute-start | bytes 6152 | tf_op jit(solution)/shard_map/ppermute | solution.py:73
  187.6 7.0 %collective-permute-start.13 = (f32[2,4,16,4]{3,2,1,0:T(8,128)S(1)}, f32[2,4,16,4]{3,2,1,0:T(8,128)S(1)}, u32[]{:S(2)}, u32[]{:S(2)}) collective-permute-start(f32[2,4,16,4]{3,2,1,0:T(8,128)S(1)} %get-tuple-element.40), channel_id=1, source_target_pairs={{1,0},{3,2},{5,4},{7,6},{9,8},{11,10},{13,12},{15,14},{17,16},{19,... | collective-permute-start | bytes 6152 | tf_op jit(solution)/shard_map/ppermute | solution.py:75
  194.7 5.5 %collective-permute-start.14 = (f32[2,4,4,72]{3,2,1,0:T(4,128)S(1)}, f32[2,4,4,72]{3,2,1,0:T(4,128)S(1)}, u32[]{:S(2)}, u32[]{:S(2)}) collective-permute-start(f32[2,4,4,72]{3,2,1,0:T(4,128)S(1)} %get-tuple-element.37), channel_id=1, source_target_pairs={{0,2},{2,4},{4,6},{6,8},{8,10},{10,12},{12,14},{14,16},{16,18},{18... | collective-permute-start | bytes 27656 | tf_op jit(solution)/shard_map/ppermute | solution.py:73
  198.2 5.1 %collective-permute-start.15 = (f32[2,4,4,72]{3,2,1,0:T(4,128)S(1)}, f32[2,4,4,72]{3,2,1,0:T(4,128)S(1)}, u32[]{:S(2)}, u32[]{:S(2)}) collective-permute-start(f32[2,4,4,72]{3,2,1,0:T(4,128)S(1)} %get-tuple-element.38), channel_id=1, source_target_pairs={{2,0},{4,2},{6,4},{8,6},{10,8},{12,10},{14,12},{16,14},{18,16},{20... | collective-permute-start | bytes 27656 | tf_op jit(solution)/shard_map/ppermute | solution.py:75
  203.4 4.9 %collective-permute-start.16 = (f32[2,4,24,72]{3,2,1,0:T(8,128)S(1)}, f32[2,4,24,72]{3,2,1,0:T(8,128)S(1)}, u32[]{:S(2)}, u32[]{:S(2)}) collective-permute-start(f32[2,4,24,72]{3,2,1,0:T(8,128)S(1)} %pad_maximum_fusion.18), channel_id=1, source_target_pairs={{0,32},{32,64},{64,96},{1,33},{33,65},{65,97},{2,34},{34,66},{66,9... | collective-permute-start | bytes 165896 | tf_op jit(solution)/shard_map/ppermute | solution.py:73
  206.7 5.4 %collective-permute-start.17 = (f32[2,4,24,72]{3,2,1,0:T(8,128)S(1)}, f32[2,4,24,72]{3,2,1,0:T(8,128)S(1)}, u32[]{:S(2)}, u32[]{:S(2)}) collective-permute-start(f32[2,4,24,72]{3,2,1,0:T(8,128)S(1)} %pad_maximum_fusion.18), channel_id=1, source_target_pairs={{32,0},{64,32},{96,64},{33,1},{65,33},{97,65},{34,2},{66,34},{98,6... | collective-permute-start | bytes 165896 | tf_op jit(solution)/shard_map/ppermute | solution.py:75
  (15 other events, 107.3 us)
